TPU v7x, 512 devices: a whole 4x8x8 slice. The times are simulated.
512 devices in a mesh: shift: 4 (over x_hi, core), space: 128 (over y, z, x_lo).
Axes of the slice: x: 4 (x_hi: 2, x_lo: 2; x = x_hi * 2 + x_lo), y: 8, z: 8, core: 2. Of those that a mesh axis runs over, the one named last changes fastest.
Arguments:
- labels: int32 [256, 32, 256], P('space'), may hold values from 0 to 7
- conductance: float32 [8], replicated, may hold values from 0.2 to 5
- capacity_table: float32 [8], replicated, may hold values from 0.5 to 2
- shift_values: float32 [8], replicated, may hold values from 0.1 to 4
- prior_basis: float32 [256, 256, 32, 256], P(None, 'space', 'shift'), may hold values from -6 to 6
Outputs:
- new_block: float32 [8, 8, 256, 32, 256], P(None, None, 'space', 'shift')
- coefficients: float32 [64, 256], replicated
- factor: float32 [64, 64], replicated
All inputs are finite; a program needn't handle non-finite values.
Results may differ from a plain program's by a relative error of at most 0.0003.
Values sent between devices are 32-bit elements; how exact they have to be, the bound alone decides.
No kernel may reach another device: no remote copies, remote signals or barrier semaphores. Data moves between devices by JAX's collectives and lax.ppermute only.
A program may use at most 64 MiB of HBM per device.

v0:
```python
import jax
import jax.numpy as jnp
from jax import lax
from jax.sharding import PartitionSpec as P

COLS = 8
SWEEPS = 4


LOWER_BOUND = 0.1
UPPER_BOUND = 2.0


def padded_2(cells, sides, width):
    for axis, dim in sides:
        count = lax.axis_size(axis)
        ends = count - 1
        head = lax.slice_in_dim(cells, 0, width, axis=dim)
        tail = lax.slice_in_dim(cells, cells.shape[dim] - width, cells.shape[dim], axis=dim)
        cells = jnp.concatenate(
            [
                lax.ppermute(tail, axis, [(i, (i + 1) % count) for i in range(ends)]),
                cells,
                lax.ppermute(head, axis, [((i + 1) % count, i) for i in range(ends)]),
            ],
            axis=dim,
        )
    return cells


def lookup(labels, table):
    materials = jnp.arange(table.shape[0], dtype=jnp.int32)
    onehot = (labels[None] == materials[:, None, None, None]).astype(jnp.float32)
    return jnp.sum(onehot * table[:, None, None, None], axis=0)


def conductances(conduct, padded):
    west_face = 0.5 * (conduct + padded[:-2, 1:-1, 1:-1])
    east_face = 0.5 * (conduct + padded[2:, 1:-1, 1:-1])
    south_face = 0.5 * (conduct + padded[1:-1, :-2, 1:-1])
    north_face = 0.5 * (conduct + padded[1:-1, 2:, 1:-1])
    below_face = 0.5 * (conduct + padded[1:-1, 1:-1, :-2])
    above_face = 0.5 * (conduct + padded[1:-1, 1:-1, 2:])
    return (west_face, east_face, south_face, north_face, below_face, above_face)


def neighbours(padded, face_list):
    west_face, east_face, south_face, north_face, below_face, above_face = face_list
    summed = west_face * padded[..., :-2, 1:-1, 1:-1] + east_face * padded[..., 2:, 1:-1, 1:-1]
    summed = (
        summed
        + south_face * padded[..., 1:-1, :-2, 1:-1]
        + north_face * padded[..., 1:-1, 2:, 1:-1]
    )
    summed = (
        summed
        + below_face * padded[..., 1:-1, 1:-1, :-2]
        + above_face * padded[..., 1:-1, 1:-1, 2:]
    )
    return summed


def diagonal_of(face_list, shift_list, capacity):
    west_face, east_face, south_face, north_face, below_face, above_face = face_list
    summed = west_face + east_face + (south_face + north_face) + (below_face + above_face)
    return summed[None, None] + shift_list[:, None, None, None, None] * capacity[None, None]


def chebyshev(source, face_list, diagonal, padder):
    center = 0.5 * (UPPER_BOUND + LOWER_BOUND)
    spread = 0.5 * (UPPER_BOUND - LOWER_BOUND)
    ratio_value = center / spread
    reciprocal = 1.0 / diagonal
    solution = jnp.zeros_like(source)
    remainder = source
    weight_old = 1.0 / ratio_value
    direction = reciprocal * remainder / center
    for sweep_index in range(SWEEPS):
        solution = solution + direction
        if sweep_index + 1 < SWEEPS:
            applied = diagonal * direction - neighbours(padder(direction), face_list)
            remainder = remainder - applied
            weight_new = 1.0 / (2.0 * ratio_value - weight_old)
            direction = weight_new * weight_old * direction + 2.0 * weight_new / spread * (
                reciprocal * remainder
            )
            weight_old = weight_new
    return solution


def products(left_side, right_side):
    return lax.dot_general(
        left_side, right_side, (((1,), (1,)), ((), ())), precision=lax.Precision.HIGHEST
    )


def matmul(left_side, right_side):
    return jnp.dot(left_side, right_side, precision=lax.Precision.HIGHEST)


def local(labels, conductance, capacity_table, shift_values, prior_basis):
    groups = lax.axis_size("shift")
    shifts_all = shift_values.shape[0]
    per_device = shifts_all // groups
    new_count = shifts_all * COLS
    basis_count = prior_basis.shape[0]
    slab_x = prior_basis.shape[1]
    quarter = prior_basis.shape[2]
    depth = prior_basis.shape[3]
    flat_basis = prior_basis.reshape(basis_count, slab_x * quarter * depth)
    cell_weight = 1.0 / (slab_x * quarter * depth * groups * lax.axis_size("space"))
    tail_columns = prior_basis[basis_count - new_count :]
    conduct = lookup(labels, conductance)
    capacity = lookup(labels, capacity_table)
    rimmed = padded_2(conduct, (("space", 0),), 1)
    face_list = conductances(conduct, jnp.pad(rimmed, ((0, 0), (1, 1), (1, 1))))
    shift_list = lax.dynamic_slice_in_dim(
        shift_values, lax.axis_index("shift") * per_device, per_device, 0
    )
    diagonal = diagonal_of(face_list, shift_list, capacity)
    starting = lax.all_to_all(tail_columns, "shift", split_axis=0, concat_axis=2, tiled=True)
    full_y = starting.shape[2]
    source = starting.reshape(per_device, COLS, slab_x, full_y, depth) * capacity[None, None]

    def padder(field):
        widened = padded_2(field, (("space", 2),), 1)
        return jnp.pad(widened, ((0, 0), (0, 0), (0, 0), (1, 1), (1, 1)))

    fields = chebyshev(source, face_list, diagonal, padder)
    merged = fields.reshape(per_device * COLS, slab_x, full_y, depth)
    regrouped = lax.all_to_all(merged, "shift", split_axis=2, concat_axis=0, tiled=True)
    columns = regrouped.reshape(new_count, slab_x * quarter * depth)
    first_proj = lax.psum(products(columns, flat_basis), ("shift", "space")) * cell_weight
    columns = columns - matmul(first_proj, flat_basis)
    second_proj = lax.psum(products(columns, flat_basis), ("shift", "space")) * cell_weight
    columns = columns - matmul(second_proj, flat_basis)
    gram_matrix = lax.psum(products(columns, columns), ("shift", "space")) * cell_weight
    factor = jnp.linalg.cholesky(gram_matrix)
    orthonormal = lax.linalg.triangular_solve(factor, columns, left_side=True, lower=True)
    new_block = orthonormal.reshape(shifts_all, COLS, slab_x, quarter, depth)
    return (new_block, first_proj + second_proj, factor)


def solution(mesh):
    in_specs = (P("space", None, None), P(), P(), P(), P(None, "space", "shift", None))
    out_specs = (P(None, None, "space", "shift", None), P(), P())
    return jax.shard_map(local, mesh=mesh, in_specs=in_specs, out_specs=out_specs, check_vma=False)
```

profile of v0, /device:TPU:1, one launch (start us, length us, event | category | flops | bytes accessed | tf_op | source)
XLA Modules:
  0.0 803.1 jit_solution(15233755541338323633)
XLA Ops:
  7.2 2.3 slice.133
  9.5 10.4 %all-to-all-start = ((f32[64,2,8,256]{3,2,1,0:T(8,128)}), f32[64,2,8,256]{3,2,1,0:T(8,128)S(1)}, u32[]{:S(2)}, u32[]{:S(2)}) async-start(f32[64,2,8,256]{3,2,1,0:T(8,128)} %slice.133), calls=%async_computation | async-start | bytes 2097152 | tf_op jit(solution)/shard_map/all_to_all | solution.py:121
  19.9 0.2 select_reduce_fusion.1
  20.1 1.3 collective-permute-start
  21.4 1.3 collective-permute-start.1
  22.7 0.1 dynamic_slice.3
  22.8 10.3 %collective-permute-done = f32[1,32,256]{2,1,0:T(8,128)S(1)} collective-permute-done((f32[1,32,256]{2,1,0:T(8,128)S(1)}, f32[1,32,256]{2,1,0:T(8,128)S(1)}, u32[]{:S(2)}, u32[]{:S(2)}) %collective-permute-start) | collective-permute-done | bytes 32800 | tf_op jit(solution)/shard_map/ppermute | solution.py:22
  33.0 0.0 collective-permute-done.1
  33.0 0.1 select_maximum_fusion.6
  33.2 0.1 add_add_fusion
  33.3 0.1 multiply_add_fusion.2
  33.4 2.3 all-to-all-done
  35.7 0.1 copy.35
  35.8 0.2 fusion.37
  36.0 0.1 fusion.69
  36.1 1.9 collective-permute-start.2
  37.9 1.3 collective-permute-start.3
  39.2 20.6 %collective-permute-done.2 = f32[2,8,1,32,256]{4,3,2,1,0:T(8,128)S(1)} collective-permute-done((f32[2,8,1,32,256]{4,3,2,1,0:T(8,128)S(1)}, f32[2,8,1,32,256]{4,3,2,1,0:T(8,128)S(1)}, u32[]{:S(2)}, u32[]{:S(2)}) %collective-permute-start.2) | collective-permute-done | bytes 524320 | tf_op jit(solution)/shard_map/ppermute | solution.py:22
  59.8 0.0 collective-permute-done.3
  59.8 1.8 select_maximum_fusion.4
  61.6 1.2 multiply_add_fusion.1
  62.8 0.1 fusion.68
  62.9 4.1 collective-permute-start.4
  67.1 1.3 collective-permute-start.5
  68.4 19.6 %collective-permute-done.4 = f32[2,8,1,32,256]{4,3,2,1,0:T(8,128)S(1)} collective-permute-done((f32[2,8,1,32,256]{4,3,2,1,0:T(8,128)S(1)}, f32[2,8,1,32,256]{4,3,2,1,0:T(8,128)S(1)}, u32[]{:S(2)}, u32[]{:S(2)}) %collective-permute-start.4) | collective-permute-done | bytes 524320 | tf_op jit(solution)/shard_map/ppermute | solution.py:22
  88.0 0.0 collective-permute-done.5
  88.0 1.8 select_maximum_fusion.2
  89.8 1.2 multiply_add_fusion
  91.0 0.1 fusion.67
  91.1 4.1 collective-permute-start.6
  95.3 1.3 collective-permute-start.7
  96.6 18.6 %collective-permute-done.6 = f32[2,8,1,32,256]{4,3,2,1,0:T(8,128)S(1)} collective-permute-done((f32[2,8,1,32,256]{4,3,2,1,0:T(8,128)S(1)}, f32[2,8,1,32,256]{4,3,2,1,0:T(8,128)S(1)}, u32[]{:S(2)}, u32[]{:S(2)}) %collective-permute-start.6) | collective-permute-done | bytes 524320 | tf_op jit(solution)/shard_map/ppermute | solution.py:22
  115.1 0.0 collective-permute-done.7
  115.1 1.8 select_maximum_fusion
  117.0 1.4 fusion.9
  118.3 1.8 copy.36
  120.1 6.9 all-to-all-start.1
  127.0 0.0 all-reduce.7.cloned.1.call-start
  127.0 7.9 copy.46
  135.0 7.2 all-to-all-done.1
  142.1 0.6 copy.53
  142.8 0.1 copy.38
  142.9 0.2 reshape.60
  143.1 6.8 fusion.71
  149.9 0.0 all-reduce.7.cloned.1.call-update
  149.9 0.3 all-reduce.9.cloned.1.call-start
  150.2 267.6 %all-reduce.7.cloned.1.call-done = f32[64,256]{1,0:T(8,128)} async-done(((f32[64,256]{1,0:T(8,128)}), f32[64,256]{1,0:T(8,128)}) %all-reduce.7.cloned.1.call-update) | async-done | bytes 65552 | tf_op jit(solution)/shard_map/psum | solution.py:133
  417.8 5.0 convolution_subtract_fusion.1
  422.7 4.6 fusion.72
  427.3 0.0 all-reduce.9.cloned.1.call-update
  427.4 251.4 %all-reduce.9.cloned.1.call-done = f32[64,256]{1,0:T(8,128)} async-done(((f32[64,256]{1,0:T(8,128)}), f32[64,256]{1,0:T(8,128)}) %all-reduce.9.cloned.1.call-update) | async-done | bytes 65552 | tf_op jit(solution)/shard_map/psum | solution.py:135
  678.8 4.8 convolution_subtract_fusion
  683.6 1.0 fusion.73
  684.6 94.9 %psum.23 = f32[64,64]{0,1:T(8,128)S(1)} all-reduce(f32[64,64]{0,1:T(8,128)S(1)} %fusion.73), channel_id=1, replica_groups=mesh['shift'=4,'space'=128] {'shift','space'}, use_global_device_ids=true, to_apply=%region_4.5 | all-reduce | flops 4096 | bytes 32768 | tf_op jit(solution)/shard_map/psum | solution.py:137
  779.5 0.1 copy.40
  779.6 5.8 cholesky.16
  785.5 0.6 compare_reduce_fusion
  786.1 1.3 select_bitcast_fusion
  787.4 4.9 custom-call.6
  792.3 0.1 copy.41
  792.4 0.3 copy.47
  792.7 1.6 fusion.34
  794.3 1.3 copy.43
  795.6 0.6 multiply_add_fusion.3
  (18 shorter events, 0.1 us)
Async XLA Ops:
  7.2 12.7 %copy-start.5 = (f32[8]{0:T(128)S(1)}, f32[8]{0:T(128)}, u32[]{:S(2)}) copy-start(f32[8]{0:T(128)} %param.7) | copy-start | bytes 100
  7.2 12.7 %copy-start.4 = (f32[8]{0:T(128)S(1)}, f32[8]{0:T(128)}, u32[]{:S(2)}) copy-start(f32[8]{0:T(128)} %param.6) | copy-start | bytes 100
  7.2 12.7 %copy-start.3 = (s32[2,32,256]{2,1,0:T(8,128)S(1)}, s32[2,32,256]{2,1,0:T(8,128)}, u32[]{:S(2)}) copy-start(s32[2,32,256]{2,1,0:T(8,128)} %param.5) | copy-start | bytes 196612
  7.2 15.5 %copy-start.6 = (f32[8]{0:T(128)S(1)}, f32[8]{0:T(128)}, u32[]{:S(2)}) copy-start(f32[8]{0:T(128)} %param.8) | copy-start | bytes 100
  9.5 26.2 %all-to-all-start = ((f32[64,2,8,256]{3,2,1,0:T(8,128)}), f32[64,2,8,256]{3,2,1,0:T(8,128)S(1)}, u32[]{:S(2)}, u32[]{:S(2)}) async-start(f32[64,2,8,256]{3,2,1,0:T(8,128)} %slice.133), calls=%async_computation | async-start | bytes 2097152 | tf_op jit(solution)/shard_map/all_to_all | solution.py:121
  20.1 13.0 %collective-permute-start = (f32[1,32,256]{2,1,0:T(8,128)S(1)}, f32[1,32,256]{2,1,0:T(8,128)S(1)}, u32[]{:S(2)}, u32[]{:S(2)}) collective-permute-start(f32[1,32,256]{2,1,0:T(8,128)S(1)} %get-tuple-element.42), channel_id=1, source_target_pairs={{0,1},{1,2},{2,3},{3,4},{4,5},{5,6},{6,7},{7,8},{8,9},{9,10},{10,1... | collective-permute-start | bytes 98312 | tf_op jit(solution)/shard_map/ppermute | solution.py:22
  21.4 11.7 %collective-permute-start.1 = (f32[1,32,256]{2,1,0:T(8,128)S(1)}, f32[1,32,256]{2,1,0:T(8,128)S(1)}, u32[]{:S(2)}, u32[]{:S(2)}) collective-permute-start(f32[1,32,256]{2,1,0:T(8,128)S(1)} %get-tuple-element.43), channel_id=1, source_target_pairs={{1,0},{2,1},{3,2},{4,3},{5,4},{6,5},{7,6},{8,7},{9,8},{10,9},{11,1... | collective-permute-start | bytes 98312 | tf_op jit(solution)/shard_map/ppermute | solution.py:24
  36.1 23.7 %collective-permute-start.2 = (f32[2,8,1,32,256]{4,3,2,1,0:T(8,128)S(1)}, f32[2,8,1,32,256]{4,3,2,1,0:T(8,128)S(1)}, u32[]{:S(2)}, u32[]{:S(2)}) collective-permute-start(f32[2,8,1,32,256]{4,3,2,1,0:T(8,128)S(1)} %get-tuple-element.37), channel_id=1, source_target_pairs={{0,1},{1,2},{2,3},{3,4},{4,5},{5,6},{6,7},{7,8},{8,9},{9,10},{10,1... | collective-permute-start | bytes 1572872 | tf_op jit(solution)/shard_map/ppermute | solution.py:22
  37.9 21.9 %collective-permute-start.3 = (f32[2,8,1,32,256]{4,3,2,1,0:T(8,128)S(1)}, f32[2,8,1,32,256]{4,3,2,1,0:T(8,128)S(1)}, u32[]{:S(2)}, u32[]{:S(2)}) collective-permute-start(f32[2,8,1,32,256]{4,3,2,1,0:T(8,128)S(1)} %get-tuple-element.38), channel_id=1, source_target_pairs={{1,0},{2,1},{3,2},{4,3},{5,4},{6,5},{7,6},{8,7},{9,8},{10,9},{11,1... | collective-permute-start | bytes 1572872 | tf_op jit(solution)/shard_map/ppermute | solution.py:24
  62.9 25.1 %collective-permute-start.4 = (f32[2,8,1,32,256]{4,3,2,1,0:T(8,128)S(1)}, f32[2,8,1,32,256]{4,3,2,1,0:T(8,128)S(1)}, u32[]{:S(2)}, u32[]{:S(2)}) collective-permute-start(f32[2,8,1,32,256]{4,3,2,1,0:T(8,128)S(1)} %get-tuple-element.35), channel_id=1, source_target_pairs={{0,1},{1,2},{2,3},{3,4},{4,5},{5,6},{6,7},{7,8},{8,9},{9,10},{10,1... | collective-permute-start | bytes 1572872 | tf_op jit(solution)/shard_map/ppermute | solution.py:22
  67.1 20.9 %collective-permute-start.5 = (f32[2,8,1,32,256]{4,3,2,1,0:T(8,128)S(1)}, f32[2,8,1,32,256]{4,3,2,1,0:T(8,128)S(1)}, u32[]{:S(2)}, u32[]{:S(2)}) collective-permute-start(f32[2,8,1,32,256]{4,3,2,1,0:T(8,128)S(1)} %get-tuple-element.36), channel_id=1, source_target_pairs={{1,0},{2,1},{3,2},{4,3},{5,4},{6,5},{7,6},{8,7},{9,8},{10,9},{11,1... | collective-permute-start | bytes 1572872 | tf_op jit(solution)/shard_map/ppermute | solution.py:24
  91.1 24.0 %collective-permute-start.6 = (f32[2,8,1,32,256]{4,3,2,1,0:T(8,128)S(1)}, f32[2,8,1,32,256]{4,3,2,1,0:T(8,128)S(1)}, u32[]{:S(2)}, u32[]{:S(2)}) collective-permute-start(f32[2,8,1,32,256]{4,3,2,1,0:T(8,128)S(1)} %get-tuple-element.33), channel_id=1, source_target_pairs={{0,1},{1,2},{2,3},{3,4},{4,5},{5,6},{6,7},{7,8},{8,9},{9,10},{10,1... | collective-permute-start | bytes 1572872 | tf_op jit(solution)/shard_map/ppermute | solution.py:22
  95.3 19.9 %collective-permute-start.7 = (f32[2,8,1,32,256]{4,3,2,1,0:T(8,128)S(1)}, f32[2,8,1,32,256]{4,3,2,1,0:T(8,128)S(1)}, u32[]{:S(2)}, u32[]{:S(2)}) collective-permute-start(f32[2,8,1,32,256]{4,3,2,1,0:T(8,128)S(1)} %get-tuple-element.34), channel_id=1, source_target_pairs={{1,0},{2,1},{3,2},{4,3},{5,4},{6,5},{7,6},{8,7},{9,8},{10,9},{11,1... | collective-permute-start | bytes 1572872 | tf_op jit(solution)/shard_map/ppermute | solution.py:24
  120.1 22.0 %all-to-all-start.1 = ((f32[16,2,32,256]{3,1,0,2:T(2,128)}), f32[16,2,32,256]{3,1,0,2:T(2,128)S(1)}, u32[]{:S(2)}, u32[]{:S(2)}) async-start(f32[16,2,32,256]{3,1,0,2:T(2,128)} %copy.36), calls=%async_computation.1 | async-start | bytes 2097152 | tf_op jit(solution)/shard_map/all_to_all | solution.py:131
  127.0 290.7 %all-reduce.7.cloned.1.call-start = ((), (), s32[]{:S(2)}) async-start(), calls=%async_computation.2 | async-start | bytes 131072 | tf_op jit(solution)/shard_map/psum | solution.py:133
  149.9 528.9 %all-reduce.9.cloned.1.call-start = ((), (), s32[]{:S(2)}) async-start(), calls=%async_computation.3 | async-start | bytes 131072 | tf_op jit(solution)/shard_map/psum | solution.py:135
  417.8 5.0 copy-start
  684.6 111.0 %copy-start.1 = (f32[64,256]{1,0:T(8,128)S(1)}, f32[64,256]{1,0:T(8,128)}, u32[]{:S(2)}) copy-start(f32[64,256]{1,0:T(8,128)} %all-reduce.7.cloned.1.call-done) | copy-start | bytes 196612
  684.6 111.0 %copy-start.2 = (f32[64,256]{1,0:T(8,128)S(1)}, f32[64,256]{1,0:T(8,128)}, u32[]{:S(2)}) copy-start(f32[64,256]{1,0:T(8,128)} %all-reduce.9.cloned.1.call-done) | copy-start | bytes 196612
Sparse Core Ops, SparseCore 0:
  150.0 267.6 all-reduce.6
  427.5 251.2 all-reduce.8
where the time goes:
time: 804 us; the launch traced here: 803 us
  waiting for transfers between devices  598 us (74%)
  blocking collectives  94.9 us (12%)
  starting transfers between devices  34.2 us (4%)
  matrix products  23.7 us (3%)
  other arithmetic  23.2 us (3%)
  local copies, waits for them, and re-layouts  15.2 us (2%)
  between operations  14.3 us (2%)
    psum x2, waiting for transfers between devices, local(): lax.psum(products(columns, flat_basis), ('shift', 'space')) * cell_weight  519 us
    psum x1, blocking collectives, local(): lax.psum(products(columns, columns), ('shift', 'space')) * cell_weight  94.9 us
    ppermute x4, waiting for transfers between devices, padded_2(): lax.ppermute(tail, axis, [(i, (i + 1) % count) for i in range(ends)])  69 us
  transfers between devices with their start and end apart: 12, of which 8 were waited for; matrix products, arithmetic and copies ran while one was open for 1% of the time, Pallas kernels for 0%

commit v1 on v0

--- a/solution.py
+++ b/solution.py
@@ -26,6 +26,17 @@
             axis=dim,
         )
     return cells
+
+
+def allsum(value):
+    axes = ("shift", "space")
+    total = lax.axis_size("shift") * lax.axis_size("space")
+    if total & (total - 1):
+        return lax.psum(value, axes)
+    for bit in range(total.bit_length() - 1):
+        mask = 1 << bit
+        value = value + lax.ppermute(value, axes, [(i, i ^ mask) for i in range(total)])
+    return value
 
 
 def lookup(labels, table):
@@ -130,11 +141,11 @@
     merged = fields.reshape(per_device * COLS, slab_x, full_y, depth)
     regrouped = lax.all_to_all(merged, "shift", split_axis=2, concat_axis=0, tiled=True)
     columns = regrouped.reshape(new_count, slab_x * quarter * depth)
-    first_proj = lax.psum(products(columns, flat_basis), ("shift", "space")) * cell_weight
+    first_proj = allsum(products(columns, flat_basis)) * cell_weight
     columns = columns - matmul(first_proj, flat_basis)
-    second_proj = lax.psum(products(columns, flat_basis), ("shift", "space")) * cell_weight
+    second_proj = allsum(products(columns, flat_basis)) * cell_weight
     columns = columns - matmul(second_proj, flat_basis)
-    gram_matrix = lax.psum(products(columns, columns), ("shift", "space")) * cell_weight
+    gram_matrix = allsum(products(columns, columns)) * cell_weight
     factor = jnp.linalg.cholesky(gram_matrix)
     orthonormal = lax.linalg.triangular_solve(factor, columns, left_side=True, lower=True)
     new_block = orthonormal.reshape(shifts_all, COLS, slab_x, quarter, depth)

time: 804 us -> 371 us (0.46)
  waiting for transfers between devices: 598 us -> 143 us
  starting transfers between devices: 34.2 us -> 169 us
  blocking collectives: 94.9 us -> 0 us
  between operations: 14.3 us -> 1.21 us
    psum x2 -> x0, waiting for transfers between devices: 519 us -> none  [local(): lax.psum(products(columns, flat_basis), ('shift', 'space')) * cell_weight]
    ppermute x0 -> x27, starting transfers between devices: none -> 135 us  [allsum(): lax.ppermute(value, axes, [(i, i ^ mask) for i in range(total)])]
    psum x1 -> x0, blocking collectives: 94.9 us -> none  [local(): lax.psum(products(columns, columns), ('shift', 'space')) * cell_weight]
    ppermute x0 -> x27, waiting for transfers between devices: none -> 64.3 us  [allsum(): lax.ppermute(value, axes, [(i, i ^ mask) for i in range(total)])]
  transfers between devices with their start and end apart: 12 -> 37, of which waited for: 8 -> 33; matrix products, arithmetic and copies ran while one was open for 1% -> 3% of each run, Pallas kernels for 0% -> 0%
where the time goes in v1:
time: 371 us; the launch traced here: 370 us
  starting transfers between devices  169 us (46%)
  waiting for transfers between devices  143 us (39%)
  other arithmetic  23.4 us (6%)
  matrix products  18.1 us (5%)
  local copies, waits for them, and re-layouts  15.3 us (4%)
    ppermute x27, starting transfers between devices, allsum(): lax.ppermute(value, axes, [(i, i ^ mask) for i in range(total)])  135 us
    ppermute x4, waiting for transfers between devices, padded_2(): lax.ppermute(tail, axis, [(i, (i + 1) % count) for i in range(ends)])  69 us
    ppermute x27, waiting for transfers between devices, allsum(): lax.ppermute(value, axes, [(i, i ^ mask) for i in range(total)])  64.3 us
    ppermute x4, starting transfers between devices, padded_2(): lax.ppermute(tail, axis, [(i, (i + 1) % count) for i in range(ends)])  11.4 us
    dot_general x3, matrix products, products(): lax.dot_general(left_side, right_side, (((1,), (1,)), ((), ())), precisio...  11.2 us
    all_to_all x1, starting transfers between devices, local(): lax.all_to_all(tail_columns, 'shift', split_axis=0, concat_axis=2, tiled=...  10.4 us
    unnamed x13, local copies, waits for them, and re-layouts  9.59 us
  transfers between devices with their start and end apart: 37, of which 33 were waited for; matrix products, arithmetic and copies ran while one was open for 3% of the time, Pallas kernels for 0%

profile of v1, /device:TPU:1, one launch (start us, length us, event | category | flops | bytes accessed | tf_op | source)
XLA Modules:
  0.0 369.8 jit_solution(17943943880740314780)
XLA Ops:
  0.7 2.3 slice.133
  3.0 10.4 %all-to-all-start = ((f32[64,2,8,256]{3,2,1,0:T(8,128)}), f32[64,2,8,256]{3,2,1,0:T(8,128)S(1)}, u32[]{:S(2)}, u32[]{:S(2)}) async-start(f32[64,2,8,256]{3,2,1,0:T(8,128)} %slice.133), calls=%async_computation | async-start | bytes 2097152 | tf_op jit(solution)/shard_map/all_to_all | solution.py:132
  16.2 10.3 %collective-permute-done = f32[1,32,256]{2,1,0:T(8,128)S(1)} collective-permute-done((f32[1,32,256]{2,1,0:T(8,128)S(1)}, f32[1,32,256]{2,1,0:T(8,128)S(1)}, u32[]{:S(2)}, u32[]{:S(2)}) %collective-permute-start) | collective-permute-done | bytes 32800 | tf_op jit(solution)/shard_map/ppermute | solution.py:22
  26.9 2.3 all-to-all-done
  29.5 1.9 collective-permute-start.2
  32.7 20.6 %collective-permute-done.2 = f32[2,8,1,32,256]{4,3,2,1,0:T(8,128)S(1)} collective-permute-done((f32[2,8,1,32,256]{4,3,2,1,0:T(8,128)S(1)}, f32[2,8,1,32,256]{4,3,2,1,0:T(8,128)S(1)}, u32[]{:S(2)}, u32[]{:S(2)}) %collective-permute-start.2) | collective-permute-done | bytes 524320 | tf_op jit(solution)/shard_map/ppermute | solution.py:22
  53.3 1.8 select_maximum_fusion.4
  56.4 4.1 %collective-permute-start.4 = (f32[2,8,1,32,256]{4,3,2,1,0:T(8,128)S(1)}, f32[2,8,1,32,256]{4,3,2,1,0:T(8,128)S(1)}, u32[]{:S(2)}, u32[]{:S(2)}) collective-permute-start(f32[2,8,1,32,256]{4,3,2,1,0:T(8,128)S(1)} %get-tuple-element.35), channel_id=1, source_target_pairs={{0,1},{1,2},{2,3},{3,4},{4,5},{5,6},{6,7},{7,8},{8,9},{9,10},{10,1... | collective-permute-start | bytes 1572872 | tf_op jit(solution)/shard_map/ppermute | solution.py:22
  61.9 19.6 %collective-permute-done.4 = f32[2,8,1,32,256]{4,3,2,1,0:T(8,128)S(1)} collective-permute-done((f32[2,8,1,32,256]{4,3,2,1,0:T(8,128)S(1)}, f32[2,8,1,32,256]{4,3,2,1,0:T(8,128)S(1)}, u32[]{:S(2)}, u32[]{:S(2)}) %collective-permute-start.4) | collective-permute-done | bytes 524320 | tf_op jit(solution)/shard_map/ppermute | solution.py:22
  81.5 1.8 select_maximum_fusion.2
  84.6 4.1 %collective-permute-start.6 = (f32[2,8,1,32,256]{4,3,2,1,0:T(8,128)S(1)}, f32[2,8,1,32,256]{4,3,2,1,0:T(8,128)S(1)}, u32[]{:S(2)}, u32[]{:S(2)}) collective-permute-start(f32[2,8,1,32,256]{4,3,2,1,0:T(8,128)S(1)} %get-tuple-element.33), channel_id=1, source_target_pairs={{0,1},{1,2},{2,3},{3,4},{4,5},{5,6},{6,7},{7,8},{8,9},{9,10},{10,1... | collective-permute-start | bytes 1572872 | tf_op jit(solution)/shard_map/ppermute | solution.py:22
  90.0 18.6 %collective-permute-done.6 = f32[2,8,1,32,256]{4,3,2,1,0:T(8,128)S(1)} collective-permute-done((f32[2,8,1,32,256]{4,3,2,1,0:T(8,128)S(1)}, f32[2,8,1,32,256]{4,3,2,1,0:T(8,128)S(1)}, u32[]{:S(2)}, u32[]{:S(2)}) %collective-permute-start.6) | collective-permute-done | bytes 524320 | tf_op jit(solution)/shard_map/ppermute | solution.py:22
  108.6 1.8 select_maximum_fusion
  113.6 6.9 %all-to-all-start.1 = ((f32[16,2,32,256]{3,1,0,2:T(2,128)}), f32[16,2,32,256]{3,1,0,2:T(2,128)S(1)}, u32[]{:S(2)}, u32[]{:S(2)}) async-start(f32[16,2,32,256]{3,1,0,2:T(2,128)} %copy.40), calls=%async_computation.1 | async-start | bytes 2097152 | tf_op jit(solution)/shard_map/all_to_all | solution.py:142
  120.5 8.0 %copy.51 = f32[32,8,16,256]{3,1,2,0:T(8,128)} copy(f32[32,8,16,256]{3,2,1,0:T(8,128)} %bitcast.53) | data formatting | bytes 8388608
  128.5 7.1 %all-to-all-done.1 = f32[16,2,32,256]{3,1,0,2:T(2,128)S(1)} async-done(((f32[16,2,32,256]{3,1,0,2:T(2,128)}), f32[16,2,32,256]{3,1,0,2:T(2,128)S(1)}, u32[]{:S(2)}, u32[]{:S(2)}) %all-to-all-start.1) | async-done | bytes 1048608 | tf_op jit(solution)/shard_map/all_to_all | solution.py:142
  136.6 6.3 %fusion.68 = f32[64,256]{1,0:T(8,128)S(1)} fusion(f32[64,4096]{1,0:T(8,128)S(1)} %reshape.60, f32[256,4096]{1,0:T(8,128)} %bitcast.45), kind=kOutput, calls=%fused_computation.121 | convolution fusion | flops 805306368 | bytes 5308416 | tf_op jit(solution)/shard_map/dot_general | solution.py:103
  142.9 4.1 %collective-permute-start.8 = (f32[64,256]{1,0:T(8,128)S(1)}, f32[64,256]{1,0:T(8,128)S(1)}, u32[]{:S(2)}, u32[]{:S(2)}) collective-permute-start(f32[64,256]{1,0:T(8,128)S(1)} %fusion.68), channel_id=1, source_target_pairs={{0,1},{1,0},{2,3},{3,2},{4,5},{5,4},{6,7},{7,6},{8,9},{9,8},{10,11... | collective-permute-start | bytes 196616 | tf_op jit(solution)/shard_map/ppermute | solution.py:38
  148.6 8.1 %collective-permute-start.9 = (f32[64,256]{1,0:T(8,128)S(1)}, f32[64,256]{1,0:T(8,128)S(1)}, u32[]{:S(2)}, u32[]{:S(2)}) collective-permute-start(f32[64,256]{1,0:T(8,128)S(1)} %add.253), channel_id=1, source_target_pairs={{0,2},{1,3},{2,0},{3,1},{4,6},{5,7},{6,4},{7,5},{8,10},{9,11},{10,... | collective-permute-start | bytes 196616 | tf_op jit(solution)/shard_map/ppermute | solution.py:38
  158.4 4.0 %collective-permute-start.10 = (f32[64,256]{1,0:T(8,128)S(1)}, f32[64,256]{1,0:T(8,128)S(1)}, u32[]{:S(2)}, u32[]{:S(2)}) collective-permute-start(f32[64,256]{1,0:T(8,128)S(1)} %add.254), channel_id=1, source_target_pairs={{0,4},{1,5},{2,6},{3,7},{4,0},{5,1},{6,2},{7,3},{8,12},{9,13},{10,... | collective-permute-start | bytes 196616 | tf_op jit(solution)/shard_map/ppermute | solution.py:38
  162.5 1.9 collective-permute-done.10
  164.4 11.9 %collective-permute-start.11 = (f32[64,256]{1,0:T(8,128)S(1)}, f32[64,256]{1,0:T(8,128)S(1)}, u32[]{:S(2)}, u32[]{:S(2)}) collective-permute-start(f32[64,256]{1,0:T(8,128)S(1)} %add.255), channel_id=1, source_target_pairs={{0,8},{1,9},{2,10},{3,11},{4,12},{5,13},{6,14},{7,15},{8,0},{9,1},... | collective-permute-start | bytes 196616 | tf_op jit(solution)/shard_map/ppermute | solution.py:38
  177.9 3.2 collective-permute-start.12
  181.1 2.0 collective-permute-done.12
  183.1 4.2 %collective-permute-start.13 = (f32[64,256]{1,0:T(8,128)S(1)}, f32[64,256]{1,0:T(8,128)S(1)}, u32[]{:S(2)}, u32[]{:S(2)}) collective-permute-start(f32[64,256]{1,0:T(8,128)S(1)} %add.257), channel_id=1, source_target_pairs={{0,32},{1,33},{2,34},{3,35},{4,36},{5,37},{6,38},{7,39},{8,40},{9,... | collective-permute-start | bytes 196616 | tf_op jit(solution)/shard_map/ppermute | solution.py:38
  189.2 8.0 %collective-permute-start.14 = (f32[64,256]{1,0:T(8,128)S(1)}, f32[64,256]{1,0:T(8,128)S(1)}, u32[]{:S(2)}, u32[]{:S(2)}) collective-permute-start(f32[64,256]{1,0:T(8,128)S(1)} %add.258), channel_id=1, source_target_pairs={{0,64},{1,65},{2,66},{3,67},{4,68},{5,69},{6,70},{7,71},{8,72},{9,... | collective-permute-start | bytes 196616 | tf_op jit(solution)/shard_map/ppermute | solution.py:38
  198.9 11.3 %collective-permute-start.15 = (f32[64,256]{1,0:T(8,128)S(1)}, f32[64,256]{1,0:T(8,128)S(1)}, u32[]{:S(2)}, u32[]{:S(2)}) collective-permute-start(f32[64,256]{1,0:T(8,128)S(1)} %add.259), channel_id=1, source_target_pairs={{0,128},{1,129},{2,130},{3,131},{4,132},{5,133},{6,134},{7,135},{8... | collective-permute-start | bytes 196616 | tf_op jit(solution)/shard_map/ppermute | solution.py:38
  211.1 2.3 collective-permute-start.16
  213.3 4.3 %collective-permute-done.16 = f32[64,256]{1,0:T(8,128)S(1)} collective-permute-done((f32[64,256]{1,0:T(8,128)S(1)}, f32[64,256]{1,0:T(8,128)S(1)}, u32[]{:S(2)}, u32[]{:S(2)}) %collective-permute-start.16) | collective-permute-done | bytes 65568 | tf_op jit(solution)/shard_map/ppermute | solution.py:38
  217.6 2.7 convolution_subtract_fusion.1
  220.2 3.9 %fusion.69 = f32[64,256]{1,0:T(8,128)S(1)} fusion(f32[64,4096]{1,0:T(8,128)S(1)} %convolution_subtract_fusion.1, f32[256,4096]{1,0:T(8,128)S(1)} %bitcast.47), kind=kOutput, calls=%fused_computation.122 | convolution fusion | flops 805306368 | bytes 5308416 | tf_op jit(solution)/shard_map/dot_general | solution.py:103
  224.2 1.9 collective-permute-start.17
  226.1 3.1 collective-permute-done.17
  229.2 1.9 collective-permute-start.18
  231.1 3.1 collective-permute-done.18
  234.2 1.9 collective-permute-start.19
  236.2 4.4 %collective-permute-done.19 = f32[64,256]{1,0:T(8,128)S(1)} collective-permute-done((f32[64,256]{1,0:T(8,128)S(1)}, f32[64,256]{1,0:T(8,128)S(1)}, u32[]{:S(2)}, u32[]{:S(2)}) %collective-permute-start.19) | collective-permute-done | bytes 65568 | tf_op jit(solution)/shard_map/ppermute | solution.py:38
  240.6 7.6 %collective-permute-start.20 = (f32[64,256]{1,0:T(8,128)S(1)}, f32[64,256]{1,0:T(8,128)S(1)}, u32[]{:S(2)}, u32[]{:S(2)}) collective-permute-start(f32[64,256]{1,0:T(8,128)S(1)} %add.264), channel_id=1, source_target_pairs={{0,8},{1,9},{2,10},{3,11},{4,12},{5,13},{6,14},{7,15},{8,0},{9,1},... | collective-permute-start | bytes 196616 | tf_op jit(solution)/shard_map/ppermute | solution.py:38
  249.8 2.6 collective-permute-start.21
  252.4 2.7 collective-permute-done.21
  255.1 3.4 collective-permute-start.22
  258.5 3.2 collective-permute-done.22
  261.7 7.4 %collective-permute-start.23 = (f32[64,256]{1,0:T(8,128)S(1)}, f32[64,256]{1,0:T(8,128)S(1)}, u32[]{:S(2)}, u32[]{:S(2)}) collective-permute-start(f32[64,256]{1,0:T(8,128)S(1)} %add.267), channel_id=1, source_target_pairs={{0,64},{1,65},{2,66},{3,67},{4,68},{5,69},{6,70},{7,71},{8,72},{9,... | collective-permute-start | bytes 196616 | tf_op jit(solution)/shard_map/ppermute | solution.py:38
  270.8 11.1 %collective-permute-start.24 = (f32[64,256]{1,0:T(8,128)S(1)}, f32[64,256]{1,0:T(8,128)S(1)}, u32[]{:S(2)}, u32[]{:S(2)}) collective-permute-start(f32[64,256]{1,0:T(8,128)S(1)} %add.268), channel_id=1, source_target_pairs={{0,128},{1,129},{2,130},{3,131},{4,132},{5,133},{6,134},{7,135},{8... | collective-permute-start | bytes 196616 | tf_op jit(solution)/shard_map/ppermute | solution.py:38
  282.9 2.0 collective-permute-start.25
  284.9 4.5 %collective-permute-done.25 = f32[64,256]{1,0:T(8,128)S(1)} collective-permute-done((f32[64,256]{1,0:T(8,128)S(1)}, f32[64,256]{1,0:T(8,128)S(1)}, u32[]{:S(2)}, u32[]{:S(2)}) %collective-permute-start.25) | collective-permute-done | bytes 65568 | tf_op jit(solution)/shard_map/ppermute | solution.py:38
  289.4 2.6 convolution_subtract_fusion
  293.0 1.9 collective-permute-start.26
  294.9 2.7 collective-permute-done.26
  297.7 2.0 collective-permute-start.27
  299.6 2.7 collective-permute-done.27
  302.3 1.9 collective-permute-start.28
  304.2 3.8 %collective-permute-done.28 = f32[64,64]{0,1:T(8,128)S(1)} collective-permute-done((f32[64,64]{0,1:T(8,128)S(1)}, f32[64,64]{0,1:T(8,128)S(1)}, u32[]{:S(2)}, u32[]{:S(2)}) %collective-permute-start.28) | collective-permute-done | bytes 16416 | tf_op jit(solution)/shard_map/ppermute | solution.py:38
  308.0 7.3 %collective-permute-start.29 = (f32[64,64]{0,1:T(8,128)S(1)}, f32[64,64]{0,1:T(8,128)S(1)}, u32[]{:S(2)}, u32[]{:S(2)}) collective-permute-start(f32[64,64]{0,1:T(8,128)S(1)} %add.273), channel_id=1, source_target_pairs={{0,8},{1,9},{2,10},{3,11},{4,12},{5,13},{6,14},{7,15},{8,0},{9,1},... | collective-permute-start | bytes 49160 | tf_op jit(solution)/shard_map/ppermute | solution.py:38
  316.6 2.0 collective-permute-start.30
  318.6 2.9 collective-permute-done.30
  321.6 2.9 collective-permute-start.31
  324.5 3.0 collective-permute-done.31
  327.5 7.0 %collective-permute-start.32 = (f32[64,64]{0,1:T(8,128)S(1)}, f32[64,64]{0,1:T(8,128)S(1)}, u32[]{:S(2)}, u32[]{:S(2)}) collective-permute-start(f32[64,64]{0,1:T(8,128)S(1)} %add.276), channel_id=1, source_target_pairs={{0,64},{1,65},{2,66},{3,67},{4,68},{5,69},{6,70},{7,71},{8,72},{9,... | collective-permute-start | bytes 49160 | tf_op jit(solution)/shard_map/ppermute | solution.py:38
  336.0 11.0 %collective-permute-start.33 = (f32[64,64]{0,1:T(8,128)S(1)}, f32[64,64]{0,1:T(8,128)S(1)}, u32[]{:S(2)}, u32[]{:S(2)}) collective-permute-start(f32[64,64]{0,1:T(8,128)S(1)} %add.277), channel_id=1, source_target_pairs={{0,128},{1,129},{2,130},{3,131},{4,132},{5,133},{6,134},{7,135},{8... | collective-permute-start | bytes 49160 | tf_op jit(solution)/shard_map/ppermute | solution.py:38
  347.9 2.2 collective-permute-start.34
  351.1 2.9 collective-permute-done.34
  354.1 5.8 %cholesky.16 = f32[64,64]{1,0:T(8,128)S(1)} custom-call(f32[64,64]{1,0:T(8,128)S(1)} %fusion.52), custom_call_target="Cholesky" | custom-call | tf_op jit(solution)/shard_map/jit(cholesky)/cholesky | solution.py:149
  361.9 4.9 %custom-call.6 = f32[1,64,64]{1,2,0:T(8,128)S(1)} custom-call(f32[1,64,64]{2,1,0:T(8,128)S(1)} %get-tuple-element.20), custom_call_target="InvertDiagBlocksLowerTriangular" | custom-call | tf_op jit(solution)/shard_map/triangular_solve | solution.py:150
  (85 shorter events, 38.4 us)
Async XLA Ops:
  0.6 12.7 %copy-start.3 = (f32[8]{0:T(128)S(1)}, f32[8]{0:T(128)}, u32[]{:S(2)}) copy-start(f32[8]{0:T(128)} %param.7) | copy-start | bytes 100
  0.6 12.7 %copy-start.2 = (f32[8]{0:T(128)S(1)}, f32[8]{0:T(128)}, u32[]{:S(2)}) copy-start(f32[8]{0:T(128)} %param.6) | copy-start | bytes 100
  0.7 12.7 %copy-start.1 = (s32[2,32,256]{2,1,0:T(8,128)S(1)}, s32[2,32,256]{2,1,0:T(8,128)}, u32[]{:S(2)}) copy-start(s32[2,32,256]{2,1,0:T(8,128)} %param.5) | copy-start | bytes 196612
  0.7 15.5 %copy-start.4 = (f32[8]{0:T(128)S(1)}, f32[8]{0:T(128)}, u32[]{:S(2)}) copy-start(f32[8]{0:T(128)} %param.8) | copy-start | bytes 100
  3.0 26.2 %all-to-all-start = ((f32[64,2,8,256]{3,2,1,0:T(8,128)}), f32[64,2,8,256]{3,2,1,0:T(8,128)S(1)}, u32[]{:S(2)}, u32[]{:S(2)}) async-start(f32[64,2,8,256]{3,2,1,0:T(8,128)} %slice.133), calls=%async_computation | async-start | bytes 2097152 | tf_op jit(solution)/shard_map/all_to_all | solution.py:132
  13.5 13.0 %collective-permute-start = (f32[1,32,256]{2,1,0:T(8,128)S(1)}, f32[1,32,256]{2,1,0:T(8,128)S(1)}, u32[]{:S(2)}, u32[]{:S(2)}) collective-permute-start(f32[1,32,256]{2,1,0:T(8,128)S(1)} %get-tuple-element.42), channel_id=1, source_target_pairs={{0,1},{1,2},{2,3},{3,4},{4,5},{5,6},{6,7},{7,8},{8,9},{9,10},{10,1... | collective-permute-start | bytes 98312 | tf_op jit(solution)/shard_map/ppermute | solution.py:22
  14.8 11.7 %collective-permute-start.1 = (f32[1,32,256]{2,1,0:T(8,128)S(1)}, f32[1,32,256]{2,1,0:T(8,128)S(1)}, u32[]{:S(2)}, u32[]{:S(2)}) collective-permute-start(f32[1,32,256]{2,1,0:T(8,128)S(1)} %get-tuple-element.43), channel_id=1, source_target_pairs={{1,0},{2,1},{3,2},{4,3},{5,4},{6,5},{7,6},{8,7},{9,8},{10,9},{11,1... | collective-permute-start | bytes 98312 | tf_op jit(solution)/shard_map/ppermute | solution.py:24
  29.5 23.7 %collective-permute-start.2 = (f32[2,8,1,32,256]{4,3,2,1,0:T(8,128)S(1)}, f32[2,8,1,32,256]{4,3,2,1,0:T(8,128)S(1)}, u32[]{:S(2)}, u32[]{:S(2)}) collective-permute-start(f32[2,8,1,32,256]{4,3,2,1,0:T(8,128)S(1)} %get-tuple-element.37), channel_id=1, source_target_pairs={{0,1},{1,2},{2,3},{3,4},{4,5},{5,6},{6,7},{7,8},{8,9},{9,10},{10,1... | collective-permute-start | bytes 1572872 | tf_op jit(solution)/shard_map/ppermute | solution.py:22
  31.4 21.9 %collective-permute-start.3 = (f32[2,8,1,32,256]{4,3,2,1,0:T(8,128)S(1)}, f32[2,8,1,32,256]{4,3,2,1,0:T(8,128)S(1)}, u32[]{:S(2)}, u32[]{:S(2)}) collective-permute-start(f32[2,8,1,32,256]{4,3,2,1,0:T(8,128)S(1)} %get-tuple-element.38), channel_id=1, source_target_pairs={{1,0},{2,1},{3,2},{4,3},{5,4},{6,5},{7,6},{8,7},{9,8},{10,9},{11,1... | collective-permute-start | bytes 1572872 | tf_op jit(solution)/shard_map/ppermute | solution.py:24
  56.4 25.1 %collective-permute-start.4 = (f32[2,8,1,32,256]{4,3,2,1,0:T(8,128)S(1)}, f32[2,8,1,32,256]{4,3,2,1,0:T(8,128)S(1)}, u32[]{:S(2)}, u32[]{:S(2)}) collective-permute-start(f32[2,8,1,32,256]{4,3,2,1,0:T(8,128)S(1)} %get-tuple-element.35), channel_id=1, source_target_pairs={{0,1},{1,2},{2,3},{3,4},{4,5},{5,6},{6,7},{7,8},{8,9},{9,10},{10,1... | collective-permute-start | bytes 1572872 | tf_op jit(solution)/shard_map/ppermute | solution.py:22
  60.6 20.9 %collective-permute-start.5 = (f32[2,8,1,32,256]{4,3,2,1,0:T(8,128)S(1)}, f32[2,8,1,32,256]{4,3,2,1,0:T(8,128)S(1)}, u32[]{:S(2)}, u32[]{:S(2)}) collective-permute-start(f32[2,8,1,32,256]{4,3,2,1,0:T(8,128)S(1)} %get-tuple-element.36), channel_id=1, source_target_pairs={{1,0},{2,1},{3,2},{4,3},{5,4},{6,5},{7,6},{8,7},{9,8},{10,9},{11,1... | collective-permute-start | bytes 1572872 | tf_op jit(solution)/shard_map/ppermute | solution.py:24
  84.6 24.0 %collective-permute-start.6 = (f32[2,8,1,32,256]{4,3,2,1,0:T(8,128)S(1)}, f32[2,8,1,32,256]{4,3,2,1,0:T(8,128)S(1)}, u32[]{:S(2)}, u32[]{:S(2)}) collective-permute-start(f32[2,8,1,32,256]{4,3,2,1,0:T(8,128)S(1)} %get-tuple-element.33), channel_id=1, source_target_pairs={{0,1},{1,2},{2,3},{3,4},{4,5},{5,6},{6,7},{7,8},{8,9},{9,10},{10,1... | collective-permute-start | bytes 1572872 | tf_op jit(solution)/shard_map/ppermute | solution.py:22
  88.7 19.9 %collective-permute-start.7 = (f32[2,8,1,32,256]{4,3,2,1,0:T(8,128)S(1)}, f32[2,8,1,32,256]{4,3,2,1,0:T(8,128)S(1)}, u32[]{:S(2)}, u32[]{:S(2)}) collective-permute-start(f32[2,8,1,32,256]{4,3,2,1,0:T(8,128)S(1)} %get-tuple-element.34), channel_id=1, source_target_pairs={{1,0},{2,1},{3,2},{4,3},{5,4},{6,5},{7,6},{8,7},{9,8},{10,9},{11,1... | collective-permute-start | bytes 1572872 | tf_op jit(solution)/shard_map/ppermute | solution.py:24
  113.6 22.0 %all-to-all-start.1 = ((f32[16,2,32,256]{3,1,0,2:T(2,128)}), f32[16,2,32,256]{3,1,0,2:T(2,128)S(1)}, u32[]{:S(2)}, u32[]{:S(2)}) async-start(f32[16,2,32,256]{3,1,0,2:T(2,128)} %copy.40), calls=%async_computation.1 | async-start | bytes 2097152 | tf_op jit(solution)/shard_map/all_to_all | solution.py:142
  136.6 81.0 %copy-start = (f32[32,8,16,256]{3,1,2,0:T(8,128)S(1)}, f32[32,8,16,256]{3,1,2,0:T(8,128)}, u32[]{:S(2)}) copy-start(f32[32,8,16,256]{3,1,2,0:T(8,128)} %copy.51) | copy-start | bytes 12582916
  142.9 5.8 %collective-permute-start.8 = (f32[64,256]{1,0:T(8,128)S(1)}, f32[64,256]{1,0:T(8,128)S(1)}, u32[]{:S(2)}, u32[]{:S(2)}) collective-permute-start(f32[64,256]{1,0:T(8,128)S(1)} %fusion.68), channel_id=1, source_target_pairs={{0,1},{1,0},{2,3},{3,2},{4,5},{5,4},{6,7},{7,6},{8,9},{9,8},{10,11... | collective-permute-start | bytes 196616 | tf_op jit(solution)/shard_map/ppermute | solution.py:38
  148.6 9.8 %collective-permute-start.9 = (f32[64,256]{1,0:T(8,128)S(1)}, f32[64,256]{1,0:T(8,128)S(1)}, u32[]{:S(2)}, u32[]{:S(2)}) collective-permute-start(f32[64,256]{1,0:T(8,128)S(1)} %add.253), channel_id=1, source_target_pairs={{0,2},{1,3},{2,0},{3,1},{4,6},{5,7},{6,4},{7,5},{8,10},{9,11},{10,... | collective-permute-start | bytes 196616 | tf_op jit(solution)/shard_map/ppermute | solution.py:38
  158.4 5.9 %collective-permute-start.10 = (f32[64,256]{1,0:T(8,128)S(1)}, f32[64,256]{1,0:T(8,128)S(1)}, u32[]{:S(2)}, u32[]{:S(2)}) collective-permute-start(f32[64,256]{1,0:T(8,128)S(1)} %add.254), channel_id=1, source_target_pairs={{0,4},{1,5},{2,6},{3,7},{4,0},{5,1},{6,2},{7,3},{8,12},{9,13},{10,... | collective-permute-start | bytes 196616 | tf_op jit(solution)/shard_map/ppermute | solution.py:38
  164.4 13.5 %collective-permute-start.11 = (f32[64,256]{1,0:T(8,128)S(1)}, f32[64,256]{1,0:T(8,128)S(1)}, u32[]{:S(2)}, u32[]{:S(2)}) collective-permute-start(f32[64,256]{1,0:T(8,128)S(1)} %add.255), channel_id=1, source_target_pairs={{0,8},{1,9},{2,10},{3,11},{4,12},{5,13},{6,14},{7,15},{8,0},{9,1},... | collective-permute-start | bytes 196616 | tf_op jit(solution)/shard_map/ppermute | solution.py:38
  177.9 5.2 %collective-permute-start.12 = (f32[64,256]{1,0:T(8,128)S(1)}, f32[64,256]{1,0:T(8,128)S(1)}, u32[]{:S(2)}, u32[]{:S(2)}) collective-permute-start(f32[64,256]{1,0:T(8,128)S(1)} %add.256), channel_id=1, source_target_pairs={{0,16},{1,17},{2,18},{3,19},{4,20},{5,21},{6,22},{7,23},{8,24},{9,... | collective-permute-start | bytes 196616 | tf_op jit(solution)/shard_map/ppermute | solution.py:38
  183.1 6.0 %collective-permute-start.13 = (f32[64,256]{1,0:T(8,128)S(1)}, f32[64,256]{1,0:T(8,128)S(1)}, u32[]{:S(2)}, u32[]{:S(2)}) collective-permute-start(f32[64,256]{1,0:T(8,128)S(1)} %add.257), channel_id=1, source_target_pairs={{0,32},{1,33},{2,34},{3,35},{4,36},{5,37},{6,38},{7,39},{8,40},{9,... | collective-permute-start | bytes 196616 | tf_op jit(solution)/shard_map/ppermute | solution.py:38
  189.2 9.7 %collective-permute-start.14 = (f32[64,256]{1,0:T(8,128)S(1)}, f32[64,256]{1,0:T(8,128)S(1)}, u32[]{:S(2)}, u32[]{:S(2)}) collective-permute-start(f32[64,256]{1,0:T(8,128)S(1)} %add.258), channel_id=1, source_target_pairs={{0,64},{1,65},{2,66},{3,67},{4,68},{5,69},{6,70},{7,71},{8,72},{9,... | collective-permute-start | bytes 196616 | tf_op jit(solution)/shard_map/ppermute | solution.py:38
  198.9 12.2 %collective-permute-start.15 = (f32[64,256]{1,0:T(8,128)S(1)}, f32[64,256]{1,0:T(8,128)S(1)}, u32[]{:S(2)}, u32[]{:S(2)}) collective-permute-start(f32[64,256]{1,0:T(8,128)S(1)} %add.259), channel_id=1, source_target_pairs={{0,128},{1,129},{2,130},{3,131},{4,132},{5,133},{6,134},{7,135},{8... | collective-permute-start | bytes 196616 | tf_op jit(solution)/shard_map/ppermute | solution.py:38
  211.1 6.5 %collective-permute-start.16 = (f32[64,256]{1,0:T(8,128)S(1)}, f32[64,256]{1,0:T(8,128)S(1)}, u32[]{:S(2)}, u32[]{:S(2)}) collective-permute-start(f32[64,256]{1,0:T(8,128)S(1)} %add.260), channel_id=1, source_target_pairs={{0,256},{1,257},{2,258},{3,259},{4,260},{5,261},{6,262},{7,263},{8... | collective-permute-start | bytes 196616 | tf_op jit(solution)/shard_map/ppermute | solution.py:38
  224.2 5.0 %collective-permute-start.17 = (f32[64,256]{1,0:T(8,128)S(1)}, f32[64,256]{1,0:T(8,128)S(1)}, u32[]{:S(2)}, u32[]{:S(2)}) collective-permute-start(f32[64,256]{1,0:T(8,128)S(1)} %fusion.69), channel_id=1, source_target_pairs={{0,1},{1,0},{2,3},{3,2},{4,5},{5,4},{6,7},{7,6},{8,9},{9,8},{10,11... | collective-permute-start | bytes 196616 | tf_op jit(solution)/shard_map/ppermute | solution.py:38
  229.2 5.0 %collective-permute-start.18 = (f32[64,256]{1,0:T(8,128)S(1)}, f32[64,256]{1,0:T(8,128)S(1)}, u32[]{:S(2)}, u32[]{:S(2)}) collective-permute-start(f32[64,256]{1,0:T(8,128)S(1)} %add.262), channel_id=1, source_target_pairs={{0,2},{1,3},{2,0},{3,1},{4,6},{5,7},{6,4},{7,5},{8,10},{9,11},{10,... | collective-permute-start | bytes 196616 | tf_op jit(solution)/shard_map/ppermute | solution.py:38
  234.2 6.3 %collective-permute-start.19 = (f32[64,256]{1,0:T(8,128)S(1)}, f32[64,256]{1,0:T(8,128)S(1)}, u32[]{:S(2)}, u32[]{:S(2)}) collective-permute-start(f32[64,256]{1,0:T(8,128)S(1)} %add.263), channel_id=1, source_target_pairs={{0,4},{1,5},{2,6},{3,7},{4,0},{5,1},{6,2},{7,3},{8,12},{9,13},{10,... | collective-permute-start | bytes 196616 | tf_op jit(solution)/shard_map/ppermute | solution.py:38
  240.6 9.2 %collective-permute-start.20 = (f32[64,256]{1,0:T(8,128)S(1)}, f32[64,256]{1,0:T(8,128)S(1)}, u32[]{:S(2)}, u32[]{:S(2)}) collective-permute-start(f32[64,256]{1,0:T(8,128)S(1)} %add.264), channel_id=1, source_target_pairs={{0,8},{1,9},{2,10},{3,11},{4,12},{5,13},{6,14},{7,15},{8,0},{9,1},... | collective-permute-start | bytes 196616 | tf_op jit(solution)/shard_map/ppermute | solution.py:38
  249.8 5.3 %collective-permute-start.21 = (f32[64,256]{1,0:T(8,128)S(1)}, f32[64,256]{1,0:T(8,128)S(1)}, u32[]{:S(2)}, u32[]{:S(2)}) collective-permute-start(f32[64,256]{1,0:T(8,128)S(1)} %add.265), channel_id=1, source_target_pairs={{0,16},{1,17},{2,18},{3,19},{4,20},{5,21},{6,22},{7,23},{8,24},{9,... | collective-permute-start | bytes 196616 | tf_op jit(solution)/shard_map/ppermute | solution.py:38
  255.1 6.6 %collective-permute-start.22 = (f32[64,256]{1,0:T(8,128)S(1)}, f32[64,256]{1,0:T(8,128)S(1)}, u32[]{:S(2)}, u32[]{:S(2)}) collective-permute-start(f32[64,256]{1,0:T(8,128)S(1)} %add.266), channel_id=1, source_target_pairs={{0,32},{1,33},{2,34},{3,35},{4,36},{5,37},{6,38},{7,39},{8,40},{9,... | collective-permute-start | bytes 196616 | tf_op jit(solution)/shard_map/ppermute | solution.py:38
  261.7 9.1 %collective-permute-start.23 = (f32[64,256]{1,0:T(8,128)S(1)}, f32[64,256]{1,0:T(8,128)S(1)}, u32[]{:S(2)}, u32[]{:S(2)}) collective-permute-start(f32[64,256]{1,0:T(8,128)S(1)} %add.267), channel_id=1, source_target_pairs={{0,64},{1,65},{2,66},{3,67},{4,68},{5,69},{6,70},{7,71},{8,72},{9,... | collective-permute-start | bytes 196616 | tf_op jit(solution)/shard_map/ppermute | solution.py:38
  270.8 12.0 %collective-permute-start.24 = (f32[64,256]{1,0:T(8,128)S(1)}, f32[64,256]{1,0:T(8,128)S(1)}, u32[]{:S(2)}, u32[]{:S(2)}) collective-permute-start(f32[64,256]{1,0:T(8,128)S(1)} %add.268), channel_id=1, source_target_pairs={{0,128},{1,129},{2,130},{3,131},{4,132},{5,133},{6,134},{7,135},{8... | collective-permute-start | bytes 196616 | tf_op jit(solution)/shard_map/ppermute | solution.py:38
  282.9 6.5 %collective-permute-start.25 = (f32[64,256]{1,0:T(8,128)S(1)}, f32[64,256]{1,0:T(8,128)S(1)}, u32[]{:S(2)}, u32[]{:S(2)}) collective-permute-start(f32[64,256]{1,0:T(8,128)S(1)} %add.269), channel_id=1, source_target_pairs={{0,256},{1,257},{2,258},{3,259},{4,260},{5,261},{6,262},{7,263},{8... | collective-permute-start | bytes 196616 | tf_op jit(solution)/shard_map/ppermute | solution.py:38
  293.0 4.7 %collective-permute-start.26 = (f32[64,64]{0,1:T(8,128)S(1)}, f32[64,64]{0,1:T(8,128)S(1)}, u32[]{:S(2)}, u32[]{:S(2)}) collective-permute-start(f32[64,64]{0,1:T(8,128)S(1)} %fusion.70), channel_id=1, source_target_pairs={{0,1},{1,0},{2,3},{3,2},{4,5},{5,4},{6,7},{7,6},{8,9},{9,8},{10,11... | collective-permute-start | bytes 49160 | tf_op jit(solution)/shard_map/ppermute | solution.py:38
  297.7 4.6 %collective-permute-start.27 = (f32[64,64]{0,1:T(8,128)S(1)}, f32[64,64]{0,1:T(8,128)S(1)}, u32[]{:S(2)}, u32[]{:S(2)}) collective-permute-start(f32[64,64]{0,1:T(8,128)S(1)} %add.271), channel_id=1, source_target_pairs={{0,2},{1,3},{2,0},{3,1},{4,6},{5,7},{6,4},{7,5},{8,10},{9,11},{10,... | collective-permute-start | bytes 49160 | tf_op jit(solution)/shard_map/ppermute | solution.py:38
  302.3 5.7 %collective-permute-start.28 = (f32[64,64]{0,1:T(8,128)S(1)}, f32[64,64]{0,1:T(8,128)S(1)}, u32[]{:S(2)}, u32[]{:S(2)}) collective-permute-start(f32[64,64]{0,1:T(8,128)S(1)} %add.272), channel_id=1, source_target_pairs={{0,4},{1,5},{2,6},{3,7},{4,0},{5,1},{6,2},{7,3},{8,12},{9,13},{10,... | collective-permute-start | bytes 49160 | tf_op jit(solution)/shard_map/ppermute | solution.py:38
  308.0 8.6 %collective-permute-start.29 = (f32[64,64]{0,1:T(8,128)S(1)}, f32[64,64]{0,1:T(8,128)S(1)}, u32[]{:S(2)}, u32[]{:S(2)}) collective-permute-start(f32[64,64]{0,1:T(8,128)S(1)} %add.273), channel_id=1, source_target_pairs={{0,8},{1,9},{2,10},{3,11},{4,12},{5,13},{6,14},{7,15},{8,0},{9,1},... | collective-permute-start | bytes 49160 | tf_op jit(solution)/shard_map/ppermute | solution.py:38
  316.6 4.9 %collective-permute-start.30 = (f32[64,64]{0,1:T(8,128)S(1)}, f32[64,64]{0,1:T(8,128)S(1)}, u32[]{:S(2)}, u32[]{:S(2)}) collective-permute-start(f32[64,64]{0,1:T(8,128)S(1)} %add.274), channel_id=1, source_target_pairs={{0,16},{1,17},{2,18},{3,19},{4,20},{5,21},{6,22},{7,23},{8,24},{9,... | collective-permute-start | bytes 49160 | tf_op jit(solution)/shard_map/ppermute | solution.py:38
  321.6 5.9 %collective-permute-start.31 = (f32[64,64]{0,1:T(8,128)S(1)}, f32[64,64]{0,1:T(8,128)S(1)}, u32[]{:S(2)}, u32[]{:S(2)}) collective-permute-start(f32[64,64]{0,1:T(8,128)S(1)} %add.275), channel_id=1, source_target_pairs={{0,32},{1,33},{2,34},{3,35},{4,36},{5,37},{6,38},{7,39},{8,40},{9,... | collective-permute-start | bytes 49160 | tf_op jit(solution)/shard_map/ppermute | solution.py:38
  327.5 8.6 %collective-permute-start.32 = (f32[64,64]{0,1:T(8,128)S(1)}, f32[64,64]{0,1:T(8,128)S(1)}, u32[]{:S(2)}, u32[]{:S(2)}) collective-permute-start(f32[64,64]{0,1:T(8,128)S(1)} %add.276), channel_id=1, source_target_pairs={{0,64},{1,65},{2,66},{3,67},{4,68},{5,69},{6,70},{7,71},{8,72},{9,... | collective-permute-start | bytes 49160 | tf_op jit(solution)/shard_map/ppermute | solution.py:38
  336.0 11.8 %collective-permute-start.33 = (f32[64,64]{0,1:T(8,128)S(1)}, f32[64,64]{0,1:T(8,128)S(1)}, u32[]{:S(2)}, u32[]{:S(2)}) collective-permute-start(f32[64,64]{0,1:T(8,128)S(1)} %add.277), channel_id=1, source_target_pairs={{0,128},{1,129},{2,130},{3,131},{4,132},{5,133},{6,134},{7,135},{8... | collective-permute-start | bytes 49160 | tf_op jit(solution)/shard_map/ppermute | solution.py:38
  347.9 6.2 %collective-permute-start.34 = (f32[64,64]{0,1:T(8,128)S(1)}, f32[64,64]{0,1:T(8,128)S(1)}, u32[]{:S(2)}, u32[]{:S(2)}) collective-permute-start(f32[64,64]{0,1:T(8,128)S(1)} %add.278), channel_id=1, source_target_pairs={{0,256},{1,257},{2,258},{3,259},{4,260},{5,261},{6,262},{7,263},{8... | collective-permute-start | bytes 49160 | tf_op jit(solution)/shard_map/ppermute | solution.py:38

commit v2 on v1

--- a/solution.py
+++ b/solution.py
@@ -121,6 +121,7 @@
     flat_basis = prior_basis.reshape(basis_count, slab_x * quarter * depth)
     cell_weight = 1.0 / (slab_x * quarter * depth * groups * lax.axis_size("space"))
     tail_columns = prior_basis[basis_count - new_count :]
+    basis_gram = allsum(products(flat_basis, flat_basis)) * cell_weight
     conduct = lookup(labels, conductance)
     capacity = lookup(labels, capacity_table)
     rimmed = padded_2(conduct, (("space", 0),), 1)
@@ -142,9 +143,8 @@
     regrouped = lax.all_to_all(merged, "shift", split_axis=2, concat_axis=0, tiled=True)
     columns = regrouped.reshape(new_count, slab_x * quarter * depth)
     first_proj = allsum(products(columns, flat_basis)) * cell_weight
-    columns = columns - matmul(first_proj, flat_basis)
-    second_proj = allsum(products(columns, flat_basis)) * cell_weight
-    columns = columns - matmul(second_proj, flat_basis)
+    second_proj = first_proj - matmul(first_proj, basis_gram)
+    columns = columns - matmul(first_proj + second_proj, flat_basis)
     gram_matrix = allsum(products(columns, columns)) * cell_weight
     factor = jnp.linalg.cholesky(gram_matrix)
     orthonormal = lax.linalg.triangular_solve(factor, columns, left_side=True, lower=True)

time: 371 us -> 344 us (0.927)
  waiting for transfers between devices: 143 us -> 126 us
  starting transfers between devices: 169 us -> 153 us
    ppermute x4, waiting for transfers between devices: 69 us -> 30.8 us  [padded_2(): lax.ppermute(tail, axis, [(i, (i + 1) % count) for i in range(ends)])]
    ppermute x27, waiting for transfers between devices: 64.3 us -> 93.4 us  [allsum(): lax.ppermute(value, axes, [(i, i ^ mask) for i in range(total)])]
    ppermute x27, starting transfers between devices: 135 us -> 123 us  [allsum(): lax.ppermute(value, axes, [(i, i ^ mask) for i in range(total)])]
    all_to_all x1, waiting for transfers between devices: 7.13 us -> 0.01 us  [local(): lax.all_to_all(merged, 'shift', split_axis=2, concat_axis=0, tiled=True)]
    dot_general x3, matrix products: 11.2 us -> 15.5 us  [products(): lax.dot_general(left_side, right_side, (((1,), (1,)), ((), ())), precisio...]
    unnamed x13 -> x17, local copies, waits for them, and re-layouts: 9.59 us -> 9.59 us
  transfers between devices with their start and end apart: 37 -> 37, of which waited for: 33 -> 24; matrix products, arithmetic and copies ran while one was open for 3% -> 10% of each run, Pallas kernels for 0% -> 0%
where the time goes in v2:
time: 344 us; the launch traced here: 339 us
  starting transfers between devices  153 us (44%)
  waiting for transfers between devices  126 us (37%)
  other arithmetic  23 us (7%)
  matrix products  20 us (6%)
  local copies, waits for them, and re-layouts  15.3 us (4%)
    ppermute x27, starting transfers between devices, allsum(): lax.ppermute(value, axes, [(i, i ^ mask) for i in range(total)])  123 us
    ppermute x27, waiting for transfers between devices, allsum(): lax.ppermute(value, axes, [(i, i ^ mask) for i in range(total)])  93.4 us
    ppermute x4, waiting for transfers between devices, padded_2(): lax.ppermute(tail, axis, [(i, (i + 1) % count) for i in range(ends)])  30.8 us
    dot_general x3, matrix products, products(): lax.dot_general(left_side, right_side, (((1,), (1,)), ((), ())), precisio...  15.5 us
    all_to_all x1, starting transfers between devices, local(): lax.all_to_all(tail_columns, 'shift', split_axis=0, concat_axis=2, tiled=...  10.4 us
    unnamed x17, local copies, waits for them, and re-layouts  9.59 us
    ppermute x4, starting transfers between devices, padded_2(): lax.ppermute(tail, axis, [(i, (i + 1) % count) for i in range(ends)])  8.62 us
  transfers between devices with their start and end apart: 37, of which 24 were waited for; matrix products, arithmetic and copies ran while one was open for 10% of the time, Pallas kernels for 0%

profile of v2, /device:TPU:1, one launch (start us, length us, event | category | flops | bytes accessed | tf_op | source)
XLA Modules:
  0.0 339.3 jit_solution(10765987194333612474)
XLA Ops:
  0.7 2.3 slice.133
  3.0 10.4 %all-to-all-start = ((f32[64,2,8,256]{3,2,1,0:T(8,128)}), f32[64,2,8,256]{3,2,1,0:T(8,128)S(1)}, u32[]{:S(2)}, u32[]{:S(2)}) async-start(f32[64,2,8,256]{3,2,1,0:T(8,128)} %slice.133), calls=%async_computation | async-start | bytes 2097152 | tf_op jit(solution)/shard_map/all_to_all | solution.py:133
  16.2 10.3 %collective-permute-done = f32[1,32,256]{2,1,0:T(8,128)S(1)} collective-permute-done((f32[1,32,256]{2,1,0:T(8,128)S(1)}, f32[1,32,256]{2,1,0:T(8,128)S(1)}, u32[]{:S(2)}, u32[]{:S(2)}) %collective-permute-start) | collective-permute-done | bytes 32800 | tf_op jit(solution)/shard_map/ppermute | solution.py:22
  26.9 2.3 all-to-all-done
  29.5 1.9 collective-permute-start.2
  32.7 20.6 %collective-permute-done.2 = f32[2,8,1,32,256]{4,3,2,1,0:T(8,128)S(1)} collective-permute-done((f32[2,8,1,32,256]{4,3,2,1,0:T(8,128)S(1)}, f32[2,8,1,32,256]{4,3,2,1,0:T(8,128)S(1)}, u32[]{:S(2)}, u32[]{:S(2)}) %collective-permute-start.2) | collective-permute-done | bytes 524320 | tf_op jit(solution)/shard_map/ppermute | solution.py:22
  53.3 1.8 select_maximum_fusion.4
  56.4 4.1 %collective-permute-start.4 = (f32[2,8,1,32,256]{4,3,2,1,0:T(8,128)S(1)}, f32[2,8,1,32,256]{4,3,2,1,0:T(8,128)S(1)}, u32[]{:S(2)}, u32[]{:S(2)}) collective-permute-start(f32[2,8,1,32,256]{4,3,2,1,0:T(8,128)S(1)} %get-tuple-element.35), channel_id=1, source_target_pairs={{0,1},{1,2},{2,3},{3,4},{4,5},{5,6},{6,7},{7,8},{8,9},{9,10},{10,1... | collective-permute-start | bytes 1572872 | tf_op jit(solution)/shard_map/ppermute | solution.py:22
  60.6 1.8 collective-permute-start.5
  62.3 8.2 %fusion.5 = f32[256,256]{1,0:T(8,128)S(1)} fusion(f32[256,2,8,256]{3,2,1,0:T(8,128)S(1)} %copy-done.1), kind=kOutput, calls=%fused_computation.16 | convolution fusion | flops 3221225472 | bytes 4456448 | tf_op jit(solution)/shard_map/dot_general | solution.py:103
  70.6 4.4 %collective-permute-start.17 = (f32[256,256]{1,0:T(8,128)S(1)}, f32[256,256]{1,0:T(8,128)S(1)}, u32[]{:S(2)}, u32[]{:S(2)}) collective-permute-start(f32[256,256]{1,0:T(8,128)S(1)} %fusion.5), channel_id=1, source_target_pairs={{0,1},{1,0},{2,3},{3,2},{4,5},{5,4},{6,7},{7,6},{8,9},{9,8},{10,11... | collective-permute-start | bytes 786440 | tf_op jit(solution)/shard_map/ppermute | solution.py:38
  75.0 12.2 %collective-permute-done.17 = f32[256,256]{1,0:T(8,128)S(1)} collective-permute-done((f32[256,256]{1,0:T(8,128)S(1)}, f32[256,256]{1,0:T(8,128)S(1)}, u32[]{:S(2)}, u32[]{:S(2)}) %collective-permute-start.17) | collective-permute-done | bytes 262176 | tf_op jit(solution)/shard_map/ppermute | solution.py:38
  87.2 7.6 %collective-permute-start.18 = (f32[256,256]{1,0:T(8,128)S(1)}, f32[256,256]{1,0:T(8,128)S(1)}, u32[]{:S(2)}, u32[]{:S(2)}) collective-permute-start(f32[256,256]{1,0:T(8,128)S(1)} %add.263), channel_id=1, source_target_pairs={{0,2},{1,3},{2,0},{3,1},{4,6},{5,7},{6,4},{7,5},{8,10},{9,11},{10,... | collective-permute-start | bytes 786440 | tf_op jit(solution)/shard_map/ppermute | solution.py:38
  94.8 1.8 select_maximum_fusion.2
  101.0 7.3 %collective-permute-start.19 = (f32[256,256]{1,0:T(8,128)S(1)}, f32[256,256]{1,0:T(8,128)S(1)}, u32[]{:S(2)}, u32[]{:S(2)}) collective-permute-start(f32[256,256]{1,0:T(8,128)S(1)} %add.264), channel_id=1, source_target_pairs={{0,4},{1,5},{2,6},{3,7},{4,0},{5,1},{6,2},{7,3},{8,12},{9,13},{10,... | collective-permute-start | bytes 786440 | tf_op jit(solution)/shard_map/ppermute | solution.py:38
  108.4 20.2 %collective-permute-done.19 = f32[256,256]{1,0:T(8,128)S(1)} collective-permute-done((f32[256,256]{1,0:T(8,128)S(1)}, f32[256,256]{1,0:T(8,128)S(1)}, u32[]{:S(2)}, u32[]{:S(2)}) %collective-permute-start.19) | collective-permute-done | bytes 262176 | tf_op jit(solution)/shard_map/ppermute | solution.py:38
  128.7 14.2 %collective-permute-start.20 = (f32[256,256]{1,0:T(8,128)S(1)}, f32[256,256]{1,0:T(8,128)S(1)}, u32[]{:S(2)}, u32[]{:S(2)}) collective-permute-start(f32[256,256]{1,0:T(8,128)S(1)} %add.265), channel_id=1, source_target_pairs={{0,8},{1,9},{2,10},{3,11},{4,12},{5,13},{6,14},{7,15},{8,0},{9,1},... | collective-permute-start | bytes 786440 | tf_op jit(solution)/shard_map/ppermute | solution.py:38
  142.9 1.8 select_maximum_fusion
  146.1 1.8 copy.48
  147.9 5.7 %all-to-all-start.1 = ((f32[16,2,32,256]{3,1,0,2:T(2,128)}), f32[16,2,32,256]{3,1,0,2:T(2,128)S(1)}, u32[]{:S(2)}, u32[]{:S(2)}) async-start(f32[16,2,32,256]{3,1,0,2:T(2,128)} %copy.48), calls=%async_computation.1 | async-start | bytes 2097152 | tf_op jit(solution)/shard_map/all_to_all | solution.py:143
  153.6 3.2 collective-permute-start.21
  156.8 4.5 %collective-permute-done.21 = f32[256,256]{1,0:T(8,128)S(1)} collective-permute-done((f32[256,256]{1,0:T(8,128)S(1)}, f32[256,256]{1,0:T(8,128)S(1)}, u32[]{:S(2)}, u32[]{:S(2)}) %collective-permute-start.21) | collective-permute-done | bytes 262176 | tf_op jit(solution)/shard_map/ppermute | solution.py:38
  161.3 4.2 %collective-permute-start.22 = (f32[256,256]{1,0:T(8,128)S(1)}, f32[256,256]{1,0:T(8,128)S(1)}, u32[]{:S(2)}, u32[]{:S(2)}) collective-permute-start(f32[256,256]{1,0:T(8,128)S(1)} %add.267), channel_id=1, source_target_pairs={{0,32},{1,33},{2,34},{3,35},{4,36},{5,37},{6,38},{7,39},{8,40},{9,... | collective-permute-start | bytes 786440 | tf_op jit(solution)/shard_map/ppermute | solution.py:38
  165.6 8.0 %copy.62 = f32[32,8,16,256]{3,1,2,0:T(8,128)} copy(f32[32,8,16,256]{3,2,1,0:T(8,128)} %bitcast.49) | data formatting | bytes 8388608
  173.5 3.4 collective-permute-done.22
  176.9 8.0 %collective-permute-start.23 = (f32[256,256]{1,0:T(8,128)S(1)}, f32[256,256]{1,0:T(8,128)S(1)}, u32[]{:S(2)}, u32[]{:S(2)}) collective-permute-start(f32[256,256]{1,0:T(8,128)S(1)} %add.268), channel_id=1, source_target_pairs={{0,64},{1,65},{2,66},{3,67},{4,68},{5,69},{6,70},{7,71},{8,72},{9,... | collective-permute-start | bytes 786440 | tf_op jit(solution)/shard_map/ppermute | solution.py:38
  185.9 6.3 %fusion.78 = f32[64,256]{1,0:T(8,128)S(1)} fusion(f32[64,4096]{1,0:T(8,128)S(1)} %reshape.60, f32[256,4096]{1,0:T(8,128)} %bitcast.47), kind=kOutput, calls=%fused_computation.127 | convolution fusion | flops 805306368 | bytes 5308416 | tf_op jit(solution)/shard_map/dot_general | solution.py:103
  192.2 1.9 collective-permute-start.8
  194.1 3.3 collective-permute-done.8
  197.4 2.1 collective-permute-start.9
  199.6 4.2 %collective-permute-start.24 = (f32[256,256]{1,0:T(8,128)S(1)}, f32[256,256]{1,0:T(8,128)S(1)}, u32[]{:S(2)}, u32[]{:S(2)}) collective-permute-start(f32[256,256]{1,0:T(8,128)S(1)} %add.269), channel_id=1, source_target_pairs={{0,128},{1,129},{2,130},{3,131},{4,132},{5,133},{6,134},{7,135},{8... | collective-permute-start | bytes 786440 | tf_op jit(solution)/shard_map/ppermute | solution.py:38
  203.8 3.8 %collective-permute-start.10 = (f32[64,256]{1,0:T(8,128)S(1)}, f32[64,256]{1,0:T(8,128)S(1)}, u32[]{:S(2)}, u32[]{:S(2)}) collective-permute-start(f32[64,256]{1,0:T(8,128)S(1)} %add.255), channel_id=1, source_target_pairs={{0,4},{1,5},{2,6},{3,7},{4,0},{5,1},{6,2},{7,3},{8,12},{9,13},{10,... | collective-permute-start | bytes 196616 | tf_op jit(solution)/shard_map/ppermute | solution.py:38
  207.7 2.1 collective-permute-done.10
  209.8 3.3 collective-permute-start.11
  213.1 6.1 %collective-permute-done.11 = f32[64,256]{1,0:T(8,128)S(1)} collective-permute-done((f32[64,256]{1,0:T(8,128)S(1)}, f32[64,256]{1,0:T(8,128)S(1)}, u32[]{:S(2)}, u32[]{:S(2)}) %collective-permute-start.11) | collective-permute-done | bytes 65568 | tf_op jit(solution)/shard_map/ppermute | solution.py:38
  219.2 1.9 collective-permute-start.12
  221.1 3.1 collective-permute-done.12
  224.2 1.9 collective-permute-start.13
  226.2 5.4 %collective-permute-start.25 = (f32[256,256]{1,0:T(8,128)S(1)}, f32[256,256]{1,0:T(8,128)S(1)}, u32[]{:S(2)}, u32[]{:S(2)}) collective-permute-start(f32[256,256]{1,0:T(8,128)S(1)} %add.270), channel_id=1, source_target_pairs={{0,256},{1,257},{2,258},{3,259},{4,260},{5,261},{6,262},{7,263},{8... | collective-permute-start | bytes 786440 | tf_op jit(solution)/shard_map/ppermute | solution.py:38
  231.6 3.8 %collective-permute-start.14 = (f32[64,256]{1,0:T(8,128)S(1)}, f32[64,256]{1,0:T(8,128)S(1)}, u32[]{:S(2)}, u32[]{:S(2)}) collective-permute-start(f32[64,256]{1,0:T(8,128)S(1)} %add.259), channel_id=1, source_target_pairs={{0,64},{1,65},{2,66},{3,67},{4,68},{5,69},{6,70},{7,71},{8,72},{9,... | collective-permute-start | bytes 196616 | tf_op jit(solution)/shard_map/ppermute | solution.py:38
  235.4 5.9 %collective-permute-done.14 = f32[64,256]{1,0:T(8,128)S(1)} collective-permute-done((f32[64,256]{1,0:T(8,128)S(1)}, f32[64,256]{1,0:T(8,128)S(1)}, u32[]{:S(2)}, u32[]{:S(2)}) %collective-permute-start.14) | collective-permute-done | bytes 65568 | tf_op jit(solution)/shard_map/ppermute | solution.py:38
  241.4 9.2 %collective-permute-start.15 = (f32[64,256]{1,0:T(8,128)S(1)}, f32[64,256]{1,0:T(8,128)S(1)}, u32[]{:S(2)}, u32[]{:S(2)}) collective-permute-start(f32[64,256]{1,0:T(8,128)S(1)} %add.260), channel_id=1, source_target_pairs={{0,128},{1,129},{2,130},{3,131},{4,132},{5,133},{6,134},{7,135},{8... | collective-permute-start | bytes 196616 | tf_op jit(solution)/shard_map/ppermute | solution.py:38
  251.4 5.4 %collective-permute-start.16 = (f32[64,256]{1,0:T(8,128)S(1)}, f32[64,256]{1,0:T(8,128)S(1)}, u32[]{:S(2)}, u32[]{:S(2)}) collective-permute-start(f32[64,256]{1,0:T(8,128)S(1)} %add.261), channel_id=1, source_target_pairs={{0,256},{1,257},{2,258},{3,259},{4,260},{5,261},{6,262},{7,263},{8... | collective-permute-start | bytes 196616 | tf_op jit(solution)/shard_map/ppermute | solution.py:38
  256.8 2.2 collective-permute-done.16
  259.3 2.7 convolution_subtract_fusion
  262.9 1.9 collective-permute-start.26
  264.9 2.7 collective-permute-done.26
  267.6 1.9 collective-permute-start.27
  269.5 2.7 collective-permute-done.27
  272.3 1.9 collective-permute-start.28
  274.2 3.7 %collective-permute-done.28 = f32[64,64]{0,1:T(8,128)S(1)} collective-permute-done((f32[64,64]{0,1:T(8,128)S(1)}, f32[64,64]{0,1:T(8,128)S(1)}, u32[]{:S(2)}, u32[]{:S(2)}) %collective-permute-start.28) | collective-permute-done | bytes 16416 | tf_op jit(solution)/shard_map/ppermute | solution.py:38
  277.9 2.1 collective-permute-start.29
  280.0 6.5 %collective-permute-done.29 = f32[64,64]{0,1:T(8,128)S(1)} collective-permute-done((f32[64,64]{0,1:T(8,128)S(1)}, f32[64,64]{0,1:T(8,128)S(1)}, u32[]{:S(2)}, u32[]{:S(2)}) %collective-permute-start.29) | collective-permute-done | bytes 16416 | tf_op jit(solution)/shard_map/ppermute | solution.py:38
  286.5 1.9 collective-permute-start.30
  288.4 3.0 collective-permute-done.30
  291.4 3.2 collective-permute-start.31
  294.6 2.3 collective-permute-done.31
  297.0 2.5 collective-permute-start.32
  299.4 6.1 %collective-permute-done.32 = f32[64,64]{0,1:T(8,128)S(1)} collective-permute-done((f32[64,64]{0,1:T(8,128)S(1)}, f32[64,64]{0,1:T(8,128)S(1)}, u32[]{:S(2)}, u32[]{:S(2)}) %collective-permute-start.32) | collective-permute-done | bytes 16416 | tf_op jit(solution)/shard_map/ppermute | solution.py:38
  305.5 10.8 %collective-permute-start.33 = (f32[64,64]{0,1:T(8,128)S(1)}, f32[64,64]{0,1:T(8,128)S(1)}, u32[]{:S(2)}, u32[]{:S(2)}) collective-permute-start(f32[64,64]{0,1:T(8,128)S(1)} %add.279), channel_id=1, source_target_pairs={{0,128},{1,129},{2,130},{3,131},{4,132},{5,133},{6,134},{7,135},{8... | collective-permute-start | bytes 49160 | tf_op jit(solution)/shard_map/ppermute | solution.py:38
  317.2 4.6 %collective-permute-start.34 = (f32[64,64]{0,1:T(8,128)S(1)}, f32[64,64]{0,1:T(8,128)S(1)}, u32[]{:S(2)}, u32[]{:S(2)}) collective-permute-start(f32[64,64]{0,1:T(8,128)S(1)} %add.280), channel_id=1, source_target_pairs={{0,256},{1,257},{2,258},{3,259},{4,260},{5,261},{6,262},{7,263},{8... | collective-permute-start | bytes 49160 | tf_op jit(solution)/shard_map/ppermute | solution.py:38
  323.4 5.8 %cholesky.16 = f32[64,64]{1,0:T(8,128)S(1)} custom-call(f32[64,64]{1,0:T(8,128)S(1)} %fusion.63), custom_call_target="Cholesky" | custom-call | tf_op jit(solution)/shard_map/jit(cholesky)/cholesky | solution.py:149
  331.2 4.9 %custom-call.6 = f32[1,64,64]{1,2,0:T(8,128)S(1)} custom-call(f32[1,64,64]{2,1,0:T(8,128)S(1)} %get-tuple-element.20), custom_call_target="InvertDiagBlocksLowerTriangular" | custom-call | tf_op jit(solution)/shard_map/triangular_solve | solution.py:150
  336.2 1.6 fusion.40
  (88 shorter events, 21.2 us)
Async XLA Ops:
  0.6 12.7 %copy-start.3 = (s32[2,32,256]{2,1,0:T(8,128)S(1)}, s32[2,32,256]{2,1,0:T(8,128)}, u32[]{:S(2)}) copy-start(s32[2,32,256]{2,1,0:T(8,128)} %param.5) | copy-start | bytes 196612
  0.6 12.7 %copy-start.4 = (f32[8]{0:T(128)S(1)}, f32[8]{0:T(128)}, u32[]{:S(2)}) copy-start(f32[8]{0:T(128)} %param.6) | copy-start | bytes 100
  0.7 12.7 %copy-start.5 = (f32[8]{0:T(128)S(1)}, f32[8]{0:T(128)}, u32[]{:S(2)}) copy-start(f32[8]{0:T(128)} %param.7) | copy-start | bytes 100
  0.7 15.5 %copy-start.6 = (f32[8]{0:T(128)S(1)}, f32[8]{0:T(128)}, u32[]{:S(2)}) copy-start(f32[8]{0:T(128)} %param.8) | copy-start | bytes 100
  3.0 26.2 %all-to-all-start = ((f32[64,2,8,256]{3,2,1,0:T(8,128)}), f32[64,2,8,256]{3,2,1,0:T(8,128)S(1)}, u32[]{:S(2)}, u32[]{:S(2)}) async-start(f32[64,2,8,256]{3,2,1,0:T(8,128)} %slice.133), calls=%async_computation | async-start | bytes 2097152 | tf_op jit(solution)/shard_map/all_to_all | solution.py:133
  13.5 13.0 %collective-permute-start = (f32[1,32,256]{2,1,0:T(8,128)S(1)}, f32[1,32,256]{2,1,0:T(8,128)S(1)}, u32[]{:S(2)}, u32[]{:S(2)}) collective-permute-start(f32[1,32,256]{2,1,0:T(8,128)S(1)} %get-tuple-element.42), channel_id=1, source_target_pairs={{0,1},{1,2},{2,3},{3,4},{4,5},{5,6},{6,7},{7,8},{8,9},{9,10},{10,1... | collective-permute-start | bytes 98312 | tf_op jit(solution)/shard_map/ppermute | solution.py:22
  14.8 11.7 %collective-permute-start.1 = (f32[1,32,256]{2,1,0:T(8,128)S(1)}, f32[1,32,256]{2,1,0:T(8,128)S(1)}, u32[]{:S(2)}, u32[]{:S(2)}) collective-permute-start(f32[1,32,256]{2,1,0:T(8,128)S(1)} %get-tuple-element.43), channel_id=1, source_target_pairs={{1,0},{2,1},{3,2},{4,3},{5,4},{6,5},{7,6},{8,7},{9,8},{10,9},{11,1... | collective-permute-start | bytes 98312 | tf_op jit(solution)/shard_map/ppermute | solution.py:24
  29.5 23.7 %collective-permute-start.2 = (f32[2,8,1,32,256]{4,3,2,1,0:T(8,128)S(1)}, f32[2,8,1,32,256]{4,3,2,1,0:T(8,128)S(1)}, u32[]{:S(2)}, u32[]{:S(2)}) collective-permute-start(f32[2,8,1,32,256]{4,3,2,1,0:T(8,128)S(1)} %get-tuple-element.37), channel_id=1, source_target_pairs={{0,1},{1,2},{2,3},{3,4},{4,5},{5,6},{6,7},{7,8},{8,9},{9,10},{10,1... | collective-permute-start | bytes 1572872 | tf_op jit(solution)/shard_map/ppermute | solution.py:22
  31.4 21.9 %collective-permute-start.3 = (f32[2,8,1,32,256]{4,3,2,1,0:T(8,128)S(1)}, f32[2,8,1,32,256]{4,3,2,1,0:T(8,128)S(1)}, u32[]{:S(2)}, u32[]{:S(2)}) collective-permute-start(f32[2,8,1,32,256]{4,3,2,1,0:T(8,128)S(1)} %get-tuple-element.38), channel_id=1, source_target_pairs={{1,0},{2,1},{3,2},{4,3},{5,4},{6,5},{7,6},{8,7},{9,8},{10,9},{11,1... | collective-permute-start | bytes 1572872 | tf_op jit(solution)/shard_map/ppermute | solution.py:24
  55.1 7.2 %copy-start.1 = (f32[256,2,8,256]{3,2,1,0:T(8,128)S(1)}, f32[256,2,8,256]{3,2,1,0:T(8,128)}, u32[]{:S(2)}) copy-start(f32[256,2,8,256]{3,2,1,0:T(8,128)} %param.9) | copy-start | bytes 12582916
  56.4 38.3 %collective-permute-start.4 = (f32[2,8,1,32,256]{4,3,2,1,0:T(8,128)S(1)}, f32[2,8,1,32,256]{4,3,2,1,0:T(8,128)S(1)}, u32[]{:S(2)}, u32[]{:S(2)}) collective-permute-start(f32[2,8,1,32,256]{4,3,2,1,0:T(8,128)S(1)} %get-tuple-element.35), channel_id=1, source_target_pairs={{0,1},{1,2},{2,3},{3,4},{4,5},{5,6},{6,7},{7,8},{8,9},{9,10},{10,1... | collective-permute-start | bytes 1572872 | tf_op jit(solution)/shard_map/ppermute | solution.py:22
  60.6 34.2 %collective-permute-start.5 = (f32[2,8,1,32,256]{4,3,2,1,0:T(8,128)S(1)}, f32[2,8,1,32,256]{4,3,2,1,0:T(8,128)S(1)}, u32[]{:S(2)}, u32[]{:S(2)}) collective-permute-start(f32[2,8,1,32,256]{4,3,2,1,0:T(8,128)S(1)} %get-tuple-element.36), channel_id=1, source_target_pairs={{1,0},{2,1},{3,2},{4,3},{5,4},{6,5},{7,6},{8,7},{9,8},{10,9},{11,1... | collective-permute-start | bytes 1572872 | tf_op jit(solution)/shard_map/ppermute | solution.py:24
  70.6 16.6 %collective-permute-start.17 = (f32[256,256]{1,0:T(8,128)S(1)}, f32[256,256]{1,0:T(8,128)S(1)}, u32[]{:S(2)}, u32[]{:S(2)}) collective-permute-start(f32[256,256]{1,0:T(8,128)S(1)} %fusion.5), channel_id=1, source_target_pairs={{0,1},{1,0},{2,3},{3,2},{4,5},{5,4},{6,7},{7,6},{8,9},{9,8},{10,11... | collective-permute-start | bytes 786440 | tf_op jit(solution)/shard_map/ppermute | solution.py:38
  87.2 13.8 %collective-permute-start.18 = (f32[256,256]{1,0:T(8,128)S(1)}, f32[256,256]{1,0:T(8,128)S(1)}, u32[]{:S(2)}, u32[]{:S(2)}) collective-permute-start(f32[256,256]{1,0:T(8,128)S(1)} %add.263), channel_id=1, source_target_pairs={{0,2},{1,3},{2,0},{3,1},{4,6},{5,7},{6,4},{7,5},{8,10},{9,11},{10,... | collective-permute-start | bytes 786440 | tf_op jit(solution)/shard_map/ppermute | solution.py:38
  97.9 45.0 %collective-permute-start.6 = (f32[2,8,1,32,256]{4,3,2,1,0:T(8,128)S(1)}, f32[2,8,1,32,256]{4,3,2,1,0:T(8,128)S(1)}, u32[]{:S(2)}, u32[]{:S(2)}) collective-permute-start(f32[2,8,1,32,256]{4,3,2,1,0:T(8,128)S(1)} %get-tuple-element.33), channel_id=1, source_target_pairs={{0,1},{1,2},{2,3},{3,4},{4,5},{5,6},{6,7},{7,8},{8,9},{9,10},{10,1... | collective-permute-start | bytes 1572872 | tf_op jit(solution)/shard_map/ppermute | solution.py:22
  99.2 43.7 %collective-permute-start.7 = (f32[2,8,1,32,256]{4,3,2,1,0:T(8,128)S(1)}, f32[2,8,1,32,256]{4,3,2,1,0:T(8,128)S(1)}, u32[]{:S(2)}, u32[]{:S(2)}) collective-permute-start(f32[2,8,1,32,256]{4,3,2,1,0:T(8,128)S(1)} %get-tuple-element.34), channel_id=1, source_target_pairs={{1,0},{2,1},{3,2},{4,3},{5,4},{6,5},{7,6},{8,7},{9,8},{10,9},{11,1... | collective-permute-start | bytes 1572872 | tf_op jit(solution)/shard_map/ppermute | solution.py:24
  101.0 27.6 %collective-permute-start.19 = (f32[256,256]{1,0:T(8,128)S(1)}, f32[256,256]{1,0:T(8,128)S(1)}, u32[]{:S(2)}, u32[]{:S(2)}) collective-permute-start(f32[256,256]{1,0:T(8,128)S(1)} %add.264), channel_id=1, source_target_pairs={{0,4},{1,5},{2,6},{3,7},{4,0},{5,1},{6,2},{7,3},{8,12},{9,13},{10,... | collective-permute-start | bytes 786440 | tf_op jit(solution)/shard_map/ppermute | solution.py:38
  128.7 24.9 %collective-permute-start.20 = (f32[256,256]{1,0:T(8,128)S(1)}, f32[256,256]{1,0:T(8,128)S(1)}, u32[]{:S(2)}, u32[]{:S(2)}) collective-permute-start(f32[256,256]{1,0:T(8,128)S(1)} %add.265), channel_id=1, source_target_pairs={{0,8},{1,9},{2,10},{3,11},{4,12},{5,13},{6,14},{7,15},{8,0},{9,1},... | collective-permute-start | bytes 786440 | tf_op jit(solution)/shard_map/ppermute | solution.py:38
  147.9 37.0 %all-to-all-start.1 = ((f32[16,2,32,256]{3,1,0,2:T(2,128)}), f32[16,2,32,256]{3,1,0,2:T(2,128)S(1)}, u32[]{:S(2)}, u32[]{:S(2)}) async-start(f32[16,2,32,256]{3,1,0,2:T(2,128)} %copy.48), calls=%async_computation.1 | async-start | bytes 2097152 | tf_op jit(solution)/shard_map/all_to_all | solution.py:143
  153.6 7.7 %collective-permute-start.21 = (f32[256,256]{1,0:T(8,128)S(1)}, f32[256,256]{1,0:T(8,128)S(1)}, u32[]{:S(2)}, u32[]{:S(2)}) collective-permute-start(f32[256,256]{1,0:T(8,128)S(1)} %add.266), channel_id=1, source_target_pairs={{0,16},{1,17},{2,18},{3,19},{4,20},{5,21},{6,22},{7,23},{8,24},{9,... | collective-permute-start | bytes 786440 | tf_op jit(solution)/shard_map/ppermute | solution.py:38
  161.3 15.6 %collective-permute-start.22 = (f32[256,256]{1,0:T(8,128)S(1)}, f32[256,256]{1,0:T(8,128)S(1)}, u32[]{:S(2)}, u32[]{:S(2)}) collective-permute-start(f32[256,256]{1,0:T(8,128)S(1)} %add.267), channel_id=1, source_target_pairs={{0,32},{1,33},{2,34},{3,35},{4,36},{5,37},{6,38},{7,39},{8,40},{9,... | collective-permute-start | bytes 786440 | tf_op jit(solution)/shard_map/ppermute | solution.py:38
  176.9 22.6 %collective-permute-start.23 = (f32[256,256]{1,0:T(8,128)S(1)}, f32[256,256]{1,0:T(8,128)S(1)}, u32[]{:S(2)}, u32[]{:S(2)}) collective-permute-start(f32[256,256]{1,0:T(8,128)S(1)} %add.268), channel_id=1, source_target_pairs={{0,64},{1,65},{2,66},{3,67},{4,68},{5,69},{6,70},{7,71},{8,72},{9,... | collective-permute-start | bytes 786440 | tf_op jit(solution)/shard_map/ppermute | solution.py:38
  185.9 73.4 %copy-start = (f32[32,8,16,256]{3,1,2,0:T(8,128)S(1)}, f32[32,8,16,256]{3,1,2,0:T(8,128)}, u32[]{:S(2)}) copy-start(f32[32,8,16,256]{3,1,2,0:T(8,128)} %copy.62) | copy-start | bytes 12582916
  192.2 5.2 %collective-permute-start.8 = (f32[64,256]{1,0:T(8,128)S(1)}, f32[64,256]{1,0:T(8,128)S(1)}, u32[]{:S(2)}, u32[]{:S(2)}) collective-permute-start(f32[64,256]{1,0:T(8,128)S(1)} %fusion.78), channel_id=1, source_target_pairs={{0,1},{1,0},{2,3},{3,2},{4,5},{5,4},{6,7},{7,6},{8,9},{9,8},{10,11... | collective-permute-start | bytes 196616 | tf_op jit(solution)/shard_map/ppermute | solution.py:38
  197.4 6.4 %collective-permute-start.9 = (f32[64,256]{1,0:T(8,128)S(1)}, f32[64,256]{1,0:T(8,128)S(1)}, u32[]{:S(2)}, u32[]{:S(2)}) collective-permute-start(f32[64,256]{1,0:T(8,128)S(1)} %add.254), channel_id=1, source_target_pairs={{0,2},{1,3},{2,0},{3,1},{4,6},{5,7},{6,4},{7,5},{8,10},{9,11},{10,... | collective-permute-start | bytes 196616 | tf_op jit(solution)/shard_map/ppermute | solution.py:38
  199.6 26.5 %collective-permute-start.24 = (f32[256,256]{1,0:T(8,128)S(1)}, f32[256,256]{1,0:T(8,128)S(1)}, u32[]{:S(2)}, u32[]{:S(2)}) collective-permute-start(f32[256,256]{1,0:T(8,128)S(1)} %add.269), channel_id=1, source_target_pairs={{0,128},{1,129},{2,130},{3,131},{4,132},{5,133},{6,134},{7,135},{8... | collective-permute-start | bytes 786440 | tf_op jit(solution)/shard_map/ppermute | solution.py:38
  203.8 5.9 %collective-permute-start.10 = (f32[64,256]{1,0:T(8,128)S(1)}, f32[64,256]{1,0:T(8,128)S(1)}, u32[]{:S(2)}, u32[]{:S(2)}) collective-permute-start(f32[64,256]{1,0:T(8,128)S(1)} %add.255), channel_id=1, source_target_pairs={{0,4},{1,5},{2,6},{3,7},{4,0},{5,1},{6,2},{7,3},{8,12},{9,13},{10,... | collective-permute-start | bytes 196616 | tf_op jit(solution)/shard_map/ppermute | solution.py:38
  209.8 9.4 %collective-permute-start.11 = (f32[64,256]{1,0:T(8,128)S(1)}, f32[64,256]{1,0:T(8,128)S(1)}, u32[]{:S(2)}, u32[]{:S(2)}) collective-permute-start(f32[64,256]{1,0:T(8,128)S(1)} %add.256), channel_id=1, source_target_pairs={{0,8},{1,9},{2,10},{3,11},{4,12},{5,13},{6,14},{7,15},{8,0},{9,1},... | collective-permute-start | bytes 196616 | tf_op jit(solution)/shard_map/ppermute | solution.py:38
  219.2 5.0 %collective-permute-start.12 = (f32[64,256]{1,0:T(8,128)S(1)}, f32[64,256]{1,0:T(8,128)S(1)}, u32[]{:S(2)}, u32[]{:S(2)}) collective-permute-start(f32[64,256]{1,0:T(8,128)S(1)} %add.257), channel_id=1, source_target_pairs={{0,16},{1,17},{2,18},{3,19},{4,20},{5,21},{6,22},{7,23},{8,24},{9,... | collective-permute-start | bytes 196616 | tf_op jit(solution)/shard_map/ppermute | solution.py:38
  224.2 7.4 %collective-permute-start.13 = (f32[64,256]{1,0:T(8,128)S(1)}, f32[64,256]{1,0:T(8,128)S(1)}, u32[]{:S(2)}, u32[]{:S(2)}) collective-permute-start(f32[64,256]{1,0:T(8,128)S(1)} %add.258), channel_id=1, source_target_pairs={{0,32},{1,33},{2,34},{3,35},{4,36},{5,37},{6,38},{7,39},{8,40},{9,... | collective-permute-start | bytes 196616 | tf_op jit(solution)/shard_map/ppermute | solution.py:38
  226.2 30.6 %collective-permute-start.25 = (f32[256,256]{1,0:T(8,128)S(1)}, f32[256,256]{1,0:T(8,128)S(1)}, u32[]{:S(2)}, u32[]{:S(2)}) collective-permute-start(f32[256,256]{1,0:T(8,128)S(1)} %add.270), channel_id=1, source_target_pairs={{0,256},{1,257},{2,258},{3,259},{4,260},{5,261},{6,262},{7,263},{8... | collective-permute-start | bytes 786440 | tf_op jit(solution)/shard_map/ppermute | solution.py:38
  231.6 9.7 %collective-permute-start.14 = (f32[64,256]{1,0:T(8,128)S(1)}, f32[64,256]{1,0:T(8,128)S(1)}, u32[]{:S(2)}, u32[]{:S(2)}) collective-permute-start(f32[64,256]{1,0:T(8,128)S(1)} %add.259), channel_id=1, source_target_pairs={{0,64},{1,65},{2,66},{3,67},{4,68},{5,69},{6,70},{7,71},{8,72},{9,... | collective-permute-start | bytes 196616 | tf_op jit(solution)/shard_map/ppermute | solution.py:38
  241.4 10.1 %collective-permute-start.15 = (f32[64,256]{1,0:T(8,128)S(1)}, f32[64,256]{1,0:T(8,128)S(1)}, u32[]{:S(2)}, u32[]{:S(2)}) collective-permute-start(f32[64,256]{1,0:T(8,128)S(1)} %add.260), channel_id=1, source_target_pairs={{0,128},{1,129},{2,130},{3,131},{4,132},{5,133},{6,134},{7,135},{8... | collective-permute-start | bytes 196616 | tf_op jit(solution)/shard_map/ppermute | solution.py:38
  251.4 7.5 %collective-permute-start.16 = (f32[64,256]{1,0:T(8,128)S(1)}, f32[64,256]{1,0:T(8,128)S(1)}, u32[]{:S(2)}, u32[]{:S(2)}) collective-permute-start(f32[64,256]{1,0:T(8,128)S(1)} %add.261), channel_id=1, source_target_pairs={{0,256},{1,257},{2,258},{3,259},{4,260},{5,261},{6,262},{7,263},{8... | collective-permute-start | bytes 196616 | tf_op jit(solution)/shard_map/ppermute | solution.py:38
  259.3 3.7 %copy-start.2 = (f32[64,256]{1,0:T(8,128)}, f32[64,256]{1,0:T(8,128)S(1)}, u32[]{:S(2)}) copy-start(f32[64,256]{1,0:T(8,128)S(1)} %fusion.8) | copy-start | bytes 196612
  262.9 4.7 %collective-permute-start.26 = (f32[64,64]{0,1:T(8,128)S(1)}, f32[64,64]{0,1:T(8,128)S(1)}, u32[]{:S(2)}, u32[]{:S(2)}) collective-permute-start(f32[64,64]{0,1:T(8,128)S(1)} %fusion.79), channel_id=1, source_target_pairs={{0,1},{1,0},{2,3},{3,2},{4,5},{5,4},{6,7},{7,6},{8,9},{9,8},{10,11... | collective-permute-start | bytes 49160 | tf_op jit(solution)/shard_map/ppermute | solution.py:38
  267.6 4.6 %collective-permute-start.27 = (f32[64,64]{0,1:T(8,128)S(1)}, f32[64,64]{0,1:T(8,128)S(1)}, u32[]{:S(2)}, u32[]{:S(2)}) collective-permute-start(f32[64,64]{0,1:T(8,128)S(1)} %add.273), channel_id=1, source_target_pairs={{0,2},{1,3},{2,0},{3,1},{4,6},{5,7},{6,4},{7,5},{8,10},{9,11},{10,... | collective-permute-start | bytes 49160 | tf_op jit(solution)/shard_map/ppermute | solution.py:38
  272.3 5.6 %collective-permute-start.28 = (f32[64,64]{0,1:T(8,128)S(1)}, f32[64,64]{0,1:T(8,128)S(1)}, u32[]{:S(2)}, u32[]{:S(2)}) collective-permute-start(f32[64,64]{0,1:T(8,128)S(1)} %add.274), channel_id=1, source_target_pairs={{0,4},{1,5},{2,6},{3,7},{4,0},{5,1},{6,2},{7,3},{8,12},{9,13},{10,... | collective-permute-start | bytes 49160 | tf_op jit(solution)/shard_map/ppermute | solution.py:38
  277.9 8.6 %collective-permute-start.29 = (f32[64,64]{0,1:T(8,128)S(1)}, f32[64,64]{0,1:T(8,128)S(1)}, u32[]{:S(2)}, u32[]{:S(2)}) collective-permute-start(f32[64,64]{0,1:T(8,128)S(1)} %add.275), channel_id=1, source_target_pairs={{0,8},{1,9},{2,10},{3,11},{4,12},{5,13},{6,14},{7,15},{8,0},{9,1},... | collective-permute-start | bytes 49160 | tf_op jit(solution)/shard_map/ppermute | solution.py:38
  286.5 4.9 %collective-permute-start.30 = (f32[64,64]{0,1:T(8,128)S(1)}, f32[64,64]{0,1:T(8,128)S(1)}, u32[]{:S(2)}, u32[]{:S(2)}) collective-permute-start(f32[64,64]{0,1:T(8,128)S(1)} %add.276), channel_id=1, source_target_pairs={{0,16},{1,17},{2,18},{3,19},{4,20},{5,21},{6,22},{7,23},{8,24},{9,... | collective-permute-start | bytes 49160 | tf_op jit(solution)/shard_map/ppermute | solution.py:38
  291.4 5.5 %collective-permute-start.31 = (f32[64,64]{0,1:T(8,128)S(1)}, f32[64,64]{0,1:T(8,128)S(1)}, u32[]{:S(2)}, u32[]{:S(2)}) collective-permute-start(f32[64,64]{0,1:T(8,128)S(1)} %add.277), channel_id=1, source_target_pairs={{0,32},{1,33},{2,34},{3,35},{4,36},{5,37},{6,38},{7,39},{8,40},{9,... | collective-permute-start | bytes 49160 | tf_op jit(solution)/shard_map/ppermute | solution.py:38
  297.0 8.6 %collective-permute-start.32 = (f32[64,64]{0,1:T(8,128)S(1)}, f32[64,64]{0,1:T(8,128)S(1)}, u32[]{:S(2)}, u32[]{:S(2)}) collective-permute-start(f32[64,64]{0,1:T(8,128)S(1)} %add.278), channel_id=1, source_target_pairs={{0,64},{1,65},{2,66},{3,67},{4,68},{5,69},{6,70},{7,71},{8,72},{9,... | collective-permute-start | bytes 49160 | tf_op jit(solution)/shard_map/ppermute | solution.py:38
  305.5 11.6 %collective-permute-start.33 = (f32[64,64]{0,1:T(8,128)S(1)}, f32[64,64]{0,1:T(8,128)S(1)}, u32[]{:S(2)}, u32[]{:S(2)}) collective-permute-start(f32[64,64]{0,1:T(8,128)S(1)} %add.279), channel_id=1, source_target_pairs={{0,128},{1,129},{2,130},{3,131},{4,132},{5,133},{6,134},{7,135},{8... | collective-permute-start | bytes 49160 | tf_op jit(solution)/shard_map/ppermute | solution.py:38
  317.2 6.2 %collective-permute-start.34 = (f32[64,64]{0,1:T(8,128)S(1)}, f32[64,64]{0,1:T(8,128)S(1)}, u32[]{:S(2)}, u32[]{:S(2)}) collective-permute-start(f32[64,64]{0,1:T(8,128)S(1)} %add.280), channel_id=1, source_target_pairs={{0,256},{1,257},{2,258},{3,259},{4,260},{5,261},{6,262},{7,263},{8... | collective-permute-start | bytes 49160 | tf_op jit(solution)/shard_map/ppermute | solution.py:38

commit v3 on v2

--- a/solution.py
+++ b/solution.py
@@ -142,14 +142,23 @@
     merged = fields.reshape(per_device * COLS, slab_x, full_y, depth)
     regrouped = lax.all_to_all(merged, "shift", split_axis=2, concat_axis=0, tiled=True)
     columns = regrouped.reshape(new_count, slab_x * quarter * depth)
-    first_proj = allsum(products(columns, flat_basis)) * cell_weight
+    sums = allsum(
+        jnp.concatenate([products(columns, flat_basis), products(columns, columns)], axis=1)
+    ) * cell_weight
+    first_proj = sums[:, :basis_count]
     second_proj = first_proj - matmul(first_proj, basis_gram)
-    columns = columns - matmul(first_proj + second_proj, flat_basis)
-    gram_matrix = allsum(products(columns, columns)) * cell_weight
+    coefficients = first_proj + second_proj
+    columns = columns - matmul(coefficients, flat_basis)
+    gram_matrix = (
+        sums[:, basis_count:]
+        - products(coefficients, first_proj)
+        - products(first_proj, coefficients)
+        + products(matmul(coefficients, basis_gram), coefficients)
+    )
     factor = jnp.linalg.cholesky(gram_matrix)
     orthonormal = lax.linalg.triangular_solve(factor, columns, left_side=True, lower=True)
     new_block = orthonormal.reshape(shifts_all, COLS, slab_x, quarter, depth)
-    return (new_block, first_proj + second_proj, factor)
+    return (new_block, coefficients, factor)
 
 
 def solution(mesh):

time: 344 us -> 301 us (0.88)
  starting transfers between devices: 153 us -> 108 us
    ppermute x27 -> x18, starting transfers between devices: 123 us -> 69.6 us  [allsum(): lax.ppermute(value, axes, [(i, i ^ mask) for i in range(total)])]
    ppermute x4, waiting for transfers between devices: 0.01 us -> 22.6 us  [padded_2(): lax.ppermute(head, axis, [((i + 1) % count, i) for i in range(ends)])]
    ppermute x27 -> x18, waiting for transfers between devices: 93.4 us -> 74.6 us  [allsum(): lax.ppermute(value, axes, [(i, i ^ mask) for i in range(total)])]
    ppermute x4, starting transfers between devices: 8.62 us -> 18 us  [padded_2(): lax.ppermute(tail, axis, [(i, (i + 1) % count) for i in range(ends)])]
    ppermute x4, waiting for transfers between devices: 30.8 us -> 25.7 us  [padded_2(): lax.ppermute(tail, axis, [(i, (i + 1) % count) for i in range(ends)])]
    unnamed x17 -> x16, local copies, waits for them, and re-layouts: 9.59 us -> 10.3 us
    dot_general x3 -> x6, matrix products: 15.5 us -> 15.5 us  [products(): lax.dot_general(left_side, right_side, (((1,), (1,)), ((), ())), precisio...]
  transfers between devices with their start and end apart: 37 -> 28, of which waited for: 24 -> 19; matrix products, arithmetic and copies ran while one was open for 10% -> 10% of each run, Pallas kernels for 0% -> 0%
where the time goes in v3:
time: 301 us; the launch traced here: 296 us
  waiting for transfers between devices  126 us (42%)
  starting transfers between devices  108 us (36%)
  other arithmetic  23 us (8%)
  matrix products  20.7 us (7%)
  local copies, waits for them, and re-layouts  16 us (5%)
    ppermute x18, waiting for transfers between devices, allsum(): lax.ppermute(value, axes, [(i, i ^ mask) for i in range(total)])  74.6 us
    ppermute x18, starting transfers between devices, allsum(): lax.ppermute(value, axes, [(i, i ^ mask) for i in range(total)])  69.6 us
    ppermute x4, waiting for transfers between devices, padded_2(): lax.ppermute(tail, axis, [(i, (i + 1) % count) for i in range(ends)])  25.7 us
    ppermute x4, waiting for transfers between devices, padded_2(): lax.ppermute(head, axis, [((i + 1) % count, i) for i in range(ends)])  22.6 us
    ppermute x4, starting transfers between devices, padded_2(): lax.ppermute(tail, axis, [(i, (i + 1) % count) for i in range(ends)])  18 us
    dot_general x6, matrix products, products(): lax.dot_general(left_side, right_side, (((1,), (1,)), ((), ())), precisio...  15.5 us
    all_to_all x1, starting transfers between devices, local(): lax.all_to_all(tail_columns, 'shift', split_axis=0, concat_axis=2, tiled=...  10.4 us
    unnamed x16, local copies, waits for them, and re-layouts  10.3 us
  transfers between devices with their start and end apart: 28, of which 19 were waited for; matrix products, arithmetic and copies ran while one was open for 10% of the time, Pallas kernels for 0%

profile of v3, /device:TPU:1, one launch (start us, length us, event | category | flops | bytes accessed | tf_op | source)
XLA Modules:
  0.0 295.5 jit_solution(11289516648490044787)
XLA Ops:
  0.7 2.3 slice.139
  3.0 10.4 %all-to-all-start = ((f32[64,2,8,256]{3,2,1,0:T(8,128)}), f32[64,2,8,256]{3,2,1,0:T(8,128)S(1)}, u32[]{:S(2)}, u32[]{:S(2)}) async-start(f32[64,2,8,256]{3,2,1,0:T(8,128)} %slice.139), calls=%async_computation | async-start | bytes 2097152 | tf_op jit(solution)/shard_map/all_to_all | solution.py:133
  13.5 1.3 collective-permute-start.1
  14.8 4.0 %collective-permute-start = (f32[1,32,256]{2,1,0:T(8,128)S(1)}, f32[1,32,256]{2,1,0:T(8,128)S(1)}, u32[]{:S(2)}, u32[]{:S(2)}) collective-permute-start(f32[1,32,256]{2,1,0:T(8,128)S(1)} %get-tuple-element.42), channel_id=1, source_target_pairs={{0,1},{1,2},{2,3},{3,4},{4,5},{5,6},{6,7},{7,8},{8,9},{9,10},{10,1... | collective-permute-start | bytes 98312 | tf_op jit(solution)/shard_map/ppermute | solution.py:22
  18.9 3.4 %collective-permute-done.1 = f32[1,32,256]{2,1,0:T(8,128)S(1)} collective-permute-done((f32[1,32,256]{2,1,0:T(8,128)S(1)}, f32[1,32,256]{2,1,0:T(8,128)S(1)}, u32[]{:S(2)}, u32[]{:S(2)}) %collective-permute-start.1) | collective-permute-done | bytes 32800 | tf_op jit(solution)/shard_map/ppermute | solution.py:24
  22.4 3.4 %collective-permute-done = f32[1,32,256]{2,1,0:T(8,128)S(1)} collective-permute-done((f32[1,32,256]{2,1,0:T(8,128)S(1)}, f32[1,32,256]{2,1,0:T(8,128)S(1)}, u32[]{:S(2)}, u32[]{:S(2)}) %collective-permute-start) | collective-permute-done | bytes 32800 | tf_op jit(solution)/shard_map/ppermute | solution.py:22
  26.2 2.9 all-to-all-done
  29.5 1.3 collective-permute-start.3
  30.8 4.0 %collective-permute-start.2 = (f32[2,8,1,32,256]{4,3,2,1,0:T(8,128)S(1)}, f32[2,8,1,32,256]{4,3,2,1,0:T(8,128)S(1)}, u32[]{:S(2)}, u32[]{:S(2)}) collective-permute-start(f32[2,8,1,32,256]{4,3,2,1,0:T(8,128)S(1)} %get-tuple-element.37), channel_id=1, source_target_pairs={{0,1},{1,2},{2,3},{3,4},{4,5},{5,6},{6,7},{7,8},{8,9},{9,10},{10,1... | collective-permute-start | bytes 1572872 | tf_op jit(solution)/shard_map/ppermute | solution.py:22
  34.8 9.2 %collective-permute-done.3 = f32[2,8,1,32,256]{4,3,2,1,0:T(8,128)S(1)} collective-permute-done((f32[2,8,1,32,256]{4,3,2,1,0:T(8,128)S(1)}, f32[2,8,1,32,256]{4,3,2,1,0:T(8,128)S(1)}, u32[]{:S(2)}, u32[]{:S(2)}) %collective-permute-start.3) | collective-permute-done | bytes 524320 | tf_op jit(solution)/shard_map/ppermute | solution.py:24
  44.0 10.4 %collective-permute-done.2 = f32[2,8,1,32,256]{4,3,2,1,0:T(8,128)S(1)} collective-permute-done((f32[2,8,1,32,256]{4,3,2,1,0:T(8,128)S(1)}, f32[2,8,1,32,256]{4,3,2,1,0:T(8,128)S(1)}, u32[]{:S(2)}, u32[]{:S(2)}) %collective-permute-start.2) | collective-permute-done | bytes 524320 | tf_op jit(solution)/shard_map/ppermute | solution.py:22
  54.4 1.8 select_maximum_fusion.4
  56.2 1.2 multiply_add_fusion.1
  57.6 1.3 collective-permute-start.5
  58.9 4.8 %collective-permute-start.4 = (f32[2,8,1,32,256]{4,3,2,1,0:T(8,128)S(1)}, f32[2,8,1,32,256]{4,3,2,1,0:T(8,128)S(1)}, u32[]{:S(2)}, u32[]{:S(2)}) collective-permute-start(f32[2,8,1,32,256]{4,3,2,1,0:T(8,128)S(1)} %get-tuple-element.35), channel_id=1, source_target_pairs={{0,1},{1,2},{2,3},{3,4},{4,5},{5,6},{6,7},{7,8},{8,9},{9,10},{10,1... | collective-permute-start | bytes 1572872 | tf_op jit(solution)/shard_map/ppermute | solution.py:22
  63.6 9.9 %collective-permute-done.5 = f32[2,8,1,32,256]{4,3,2,1,0:T(8,128)S(1)} collective-permute-done((f32[2,8,1,32,256]{4,3,2,1,0:T(8,128)S(1)}, f32[2,8,1,32,256]{4,3,2,1,0:T(8,128)S(1)}, u32[]{:S(2)}, u32[]{:S(2)}) %collective-permute-start.5) | collective-permute-done | bytes 524320 | tf_op jit(solution)/shard_map/ppermute | solution.py:24
  73.5 11.9 %collective-permute-done.4 = f32[2,8,1,32,256]{4,3,2,1,0:T(8,128)S(1)} collective-permute-done((f32[2,8,1,32,256]{4,3,2,1,0:T(8,128)S(1)}, f32[2,8,1,32,256]{4,3,2,1,0:T(8,128)S(1)}, u32[]{:S(2)}, u32[]{:S(2)}) %collective-permute-start.4) | collective-permute-done | bytes 524320 | tf_op jit(solution)/shard_map/ppermute | solution.py:22
  85.4 1.8 select_maximum_fusion.2
  87.3 1.2 multiply_add_fusion
  88.6 1.3 collective-permute-start.7
  89.9 5.2 %collective-permute-start.6 = (f32[2,8,1,32,256]{4,3,2,1,0:T(8,128)S(1)}, f32[2,8,1,32,256]{4,3,2,1,0:T(8,128)S(1)}, u32[]{:S(2)}, u32[]{:S(2)}) collective-permute-start(f32[2,8,1,32,256]{4,3,2,1,0:T(8,128)S(1)} %get-tuple-element.33), channel_id=1, source_target_pairs={{0,1},{1,2},{2,3},{3,4},{4,5},{5,6},{6,7},{7,8},{8,9},{9,10},{10,1... | collective-permute-start | bytes 1572872 | tf_op jit(solution)/shard_map/ppermute | solution.py:22
  95.1 8.2 %fusion.5 = f32[256,256]{1,0:T(8,128)S(1)} fusion(f32[256,2,8,256]{3,2,1,0:T(8,128)S(1)} %copy-done.1), kind=kOutput, calls=%fused_computation.16 | convolution fusion | flops 3221225472 | bytes 4456448 | tf_op jit(solution)/shard_map/dot_general | solution.py:103
  103.3 4.2 %collective-permute-start.17 = (f32[256,256]{1,0:T(8,128)S(1)}, f32[256,256]{1,0:T(8,128)S(1)}, u32[]{:S(2)}, u32[]{:S(2)}) collective-permute-start(f32[256,256]{1,0:T(8,128)S(1)} %fusion.5), channel_id=1, source_target_pairs={{0,1},{1,0},{2,3},{3,2},{4,5},{5,4},{6,7},{7,6},{8,9},{9,8},{10,11... | collective-permute-start | bytes 786440 | tf_op jit(solution)/shard_map/ppermute | solution.py:38
  107.6 14.5 %collective-permute-done.17 = f32[256,256]{1,0:T(8,128)S(1)} collective-permute-done((f32[256,256]{1,0:T(8,128)S(1)}, f32[256,256]{1,0:T(8,128)S(1)}, u32[]{:S(2)}, u32[]{:S(2)}) %collective-permute-start.17) | collective-permute-done | bytes 262176 | tf_op jit(solution)/shard_map/ppermute | solution.py:38
  122.1 2.1 collective-permute-start.18
  124.2 1.8 select_maximum_fusion
  126.1 1.4 fusion.15
  127.4 1.8 copy.68
  129.2 5.3 %all-to-all-start.1 = ((f32[16,2,32,256]{3,1,0,2:T(2,128)}), f32[16,2,32,256]{3,1,0,2:T(2,128)S(1)}, u32[]{:S(2)}, u32[]{:S(2)}) async-start(f32[16,2,32,256]{3,1,0,2:T(2,128)} %copy.68), calls=%async_computation.1 | async-start | bytes 2097152 | tf_op jit(solution)/shard_map/all_to_all | solution.py:143
  134.6 7.1 %collective-permute-start.19 = (f32[256,256]{1,0:T(8,128)S(1)}, f32[256,256]{1,0:T(8,128)S(1)}, u32[]{:S(2)}, u32[]{:S(2)}) collective-permute-start(f32[256,256]{1,0:T(8,128)S(1)} %add.239), channel_id=1, source_target_pairs={{0,4},{1,5},{2,6},{3,7},{4,0},{5,1},{6,2},{7,3},{8,12},{9,13},{10,... | collective-permute-start | bytes 786440 | tf_op jit(solution)/shard_map/ppermute | solution.py:38
  141.6 11.9 %collective-permute-done.19 = f32[256,256]{1,0:T(8,128)S(1)} collective-permute-done((f32[256,256]{1,0:T(8,128)S(1)}, f32[256,256]{1,0:T(8,128)S(1)}, u32[]{:S(2)}, u32[]{:S(2)}) %collective-permute-start.19) | collective-permute-done | bytes 262176 | tf_op jit(solution)/shard_map/ppermute | solution.py:38
  153.6 7.5 %collective-permute-start.20 = (f32[256,256]{1,0:T(8,128)S(1)}, f32[256,256]{1,0:T(8,128)S(1)}, u32[]{:S(2)}, u32[]{:S(2)}) collective-permute-start(f32[256,256]{1,0:T(8,128)S(1)} %add.240), channel_id=1, source_target_pairs={{0,8},{1,9},{2,10},{3,11},{4,12},{5,13},{6,14},{7,15},{8,0},{9,1},... | collective-permute-start | bytes 786440 | tf_op jit(solution)/shard_map/ppermute | solution.py:38
  161.1 7.9 %copy.92 = f32[32,8,16,256]{3,1,2,0:T(8,128)} copy(f32[32,8,16,256]{3,2,1,0:T(8,128)} %bitcast.54) | data formatting | bytes 8388608
  169.1 4.0 %collective-permute-done.20 = f32[256,256]{1,0:T(8,128)S(1)} collective-permute-done((f32[256,256]{1,0:T(8,128)S(1)}, f32[256,256]{1,0:T(8,128)S(1)}, u32[]{:S(2)}, u32[]{:S(2)}) %collective-permute-start.20) | collective-permute-done | bytes 262176 | tf_op jit(solution)/shard_map/ppermute | solution.py:38
  173.1 3.2 %collective-permute-start.21 = (f32[256,256]{1,0:T(8,128)S(1)}, f32[256,256]{1,0:T(8,128)S(1)}, u32[]{:S(2)}, u32[]{:S(2)}) collective-permute-start(f32[256,256]{1,0:T(8,128)S(1)} %add.241), channel_id=1, source_target_pairs={{0,16},{1,17},{2,18},{3,19},{4,20},{5,21},{6,22},{7,23},{8,24},{9,... | collective-permute-start | bytes 786440 | tf_op jit(solution)/shard_map/ppermute | solution.py:38
  177.2 5.2 %fusion.82 = f32[64,256]{0,1:T(8,128)S(1)} fusion(f32[64,4096]{1,0:T(8,128)S(1)} %reshape.60, f32[256,4096]{1,0:T(8,128)} %bitcast.52), kind=kOutput, calls=%fused_computation.134 | convolution fusion | flops 805306368 | bytes 5308416 | tf_op jit(solution)/shard_map/dot_general | solution.py:103
  183.4 4.1 %collective-permute-start.8 = (f32[64,320]{0,1:T(8,128)S(1)}, f32[64,320]{0,1:T(8,128)S(1)}, u32[]{:S(2)}, u32[]{:S(2)}) collective-permute-start(f32[64,320]{0,1:T(8,128)S(1)} %pad_maximum_fusion.6), channel_id=1, source_target_pairs={{0,1},{1,0},{2,3},{3,2},{4,5},{5,4},{6,7},{7,6},{8,9},{9,8},{10,11... | collective-permute-start | bytes 245768 | tf_op jit(solution)/shard_map/ppermute | solution.py:38
  187.6 4.3 %collective-permute-start.22 = (f32[256,256]{1,0:T(8,128)S(1)}, f32[256,256]{1,0:T(8,128)S(1)}, u32[]{:S(2)}, u32[]{:S(2)}) collective-permute-start(f32[256,256]{1,0:T(8,128)S(1)} %add.242), channel_id=1, source_target_pairs={{0,32},{1,33},{2,34},{3,35},{4,36},{5,37},{6,38},{7,39},{8,40},{9,... | collective-permute-start | bytes 786440 | tf_op jit(solution)/shard_map/ppermute | solution.py:38
  192.0 1.9 collective-permute-start.9
  193.9 4.1 %collective-permute-done.9 = f32[64,320]{0,1:T(8,128)S(1)} collective-permute-done((f32[64,320]{0,1:T(8,128)S(1)}, f32[64,320]{0,1:T(8,128)S(1)}, u32[]{:S(2)}, u32[]{:S(2)}) %collective-permute-start.9) | collective-permute-done | bytes 81952 | tf_op jit(solution)/shard_map/ppermute | solution.py:38
  198.1 2.9 collective-permute-start.10
  201.0 3.4 %collective-permute-done.22 = f32[256,256]{1,0:T(8,128)S(1)} collective-permute-done((f32[256,256]{1,0:T(8,128)S(1)}, f32[256,256]{1,0:T(8,128)S(1)}, u32[]{:S(2)}, u32[]{:S(2)}) %collective-permute-start.22) | collective-permute-done | bytes 262176 | tf_op jit(solution)/shard_map/ppermute | solution.py:38
  204.5 5.8 %collective-permute-start.23 = (f32[256,256]{1,0:T(8,128)S(1)}, f32[256,256]{1,0:T(8,128)S(1)}, u32[]{:S(2)}, u32[]{:S(2)}) collective-permute-start(f32[256,256]{1,0:T(8,128)S(1)} %add.243), channel_id=1, source_target_pairs={{0,64},{1,65},{2,66},{3,67},{4,68},{5,69},{6,70},{7,71},{8,72},{9,... | collective-permute-start | bytes 786440 | tf_op jit(solution)/shard_map/ppermute | solution.py:38
  210.3 4.3 %collective-permute-start.11 = (f32[64,320]{0,1:T(8,128)S(1)}, f32[64,320]{0,1:T(8,128)S(1)}, u32[]{:S(2)}, u32[]{:S(2)}) collective-permute-start(f32[64,320]{0,1:T(8,128)S(1)} %add.231), channel_id=1, source_target_pairs={{0,8},{1,9},{2,10},{3,11},{4,12},{5,13},{6,14},{7,15},{8,0},{9,1},... | collective-permute-start | bytes 245768 | tf_op jit(solution)/shard_map/ppermute | solution.py:38
  214.6 8.8 %collective-permute-done.11 = f32[64,320]{0,1:T(8,128)S(1)} collective-permute-done((f32[64,320]{0,1:T(8,128)S(1)}, f32[64,320]{0,1:T(8,128)S(1)}, u32[]{:S(2)}, u32[]{:S(2)}) %collective-permute-start.11) | collective-permute-done | bytes 81952 | tf_op jit(solution)/shard_map/ppermute | solution.py:38
  223.5 1.9 collective-permute-start.12
  225.4 4.1 %collective-permute-done.12 = f32[64,320]{0,1:T(8,128)S(1)} collective-permute-done((f32[64,320]{0,1:T(8,128)S(1)}, f32[64,320]{0,1:T(8,128)S(1)}, u32[]{:S(2)}, u32[]{:S(2)}) %collective-permute-start.12) | collective-permute-done | bytes 81952 | tf_op jit(solution)/shard_map/ppermute | solution.py:38
  229.6 2.1 collective-permute-start.13
  231.7 4.9 %collective-permute-start.24 = (f32[256,256]{1,0:T(8,128)S(1)}, f32[256,256]{1,0:T(8,128)S(1)}, u32[]{:S(2)}, u32[]{:S(2)}) collective-permute-start(f32[256,256]{1,0:T(8,128)S(1)} %add.244), channel_id=1, source_target_pairs={{0,128},{1,129},{2,130},{3,131},{4,132},{5,133},{6,134},{7,135},{8... | collective-permute-start | bytes 786440 | tf_op jit(solution)/shard_map/ppermute | solution.py:38
  236.6 3.7 %collective-permute-done.13 = f32[64,320]{0,1:T(8,128)S(1)} collective-permute-done((f32[64,320]{0,1:T(8,128)S(1)}, f32[64,320]{0,1:T(8,128)S(1)}, u32[]{:S(2)}, u32[]{:S(2)}) %collective-permute-start.13) | collective-permute-done | bytes 81952 | tf_op jit(solution)/shard_map/ppermute | solution.py:38
  240.3 1.9 collective-permute-start.14
  242.2 10.3 %collective-permute-done.14 = f32[64,320]{0,1:T(8,128)S(1)} collective-permute-done((f32[64,320]{0,1:T(8,128)S(1)}, f32[64,320]{0,1:T(8,128)S(1)}, u32[]{:S(2)}, u32[]{:S(2)}) %collective-permute-start.14) | collective-permute-done | bytes 81952 | tf_op jit(solution)/shard_map/ppermute | solution.py:38
  252.6 4.4 %collective-permute-start.15 = (f32[64,320]{0,1:T(8,128)S(1)}, f32[64,320]{0,1:T(8,128)S(1)}, u32[]{:S(2)}, u32[]{:S(2)}) collective-permute-start(f32[64,320]{0,1:T(8,128)S(1)} %add.235), channel_id=1, source_target_pairs={{0,128},{1,129},{2,130},{3,131},{4,132},{5,133},{6,134},{7,135},{8... | collective-permute-start | bytes 245768 | tf_op jit(solution)/shard_map/ppermute | solution.py:38
  256.9 1.0 collective-permute-done.15
  258.0 5.1 %collective-permute-start.16 = (f32[64,320]{0,1:T(8,128)S(1)}, f32[64,320]{0,1:T(8,128)S(1)}, u32[]{:S(2)}, u32[]{:S(2)}) collective-permute-start(f32[64,320]{0,1:T(8,128)S(1)} %add.236), channel_id=1, source_target_pairs={{0,256},{1,257},{2,258},{3,259},{4,260},{5,261},{6,262},{7,263},{8... | collective-permute-start | bytes 245768 | tf_op jit(solution)/shard_map/ppermute | solution.py:38
  263.1 1.9 collective-permute-start.25
  265.0 2.2 collective-permute-done.16
  267.3 6.5 %collective-permute-done.25 = f32[256,256]{1,0:T(8,128)S(1)} collective-permute-done((f32[256,256]{1,0:T(8,128)S(1)}, f32[256,256]{1,0:T(8,128)S(1)}, u32[]{:S(2)}, u32[]{:S(2)}) %collective-permute-start.25) | collective-permute-done | bytes 262176 | tf_op jit(solution)/shard_map/ppermute | solution.py:38
  274.3 2.7 convolution_subtract_fusion
  279.6 5.8 %cholesky.16 = f32[64,64]{1,0:T(8,128)S(1)} custom-call(f32[64,64]{1,0:T(8,128)S(1)} %fusion.66), custom_call_target="Cholesky" | custom-call | tf_op jit(solution)/shard_map/jit(cholesky)/cholesky | solution.py:158
  286.2 1.3 select_bitcast_fusion
  287.4 4.9 %custom-call.6 = f32[1,64,64]{1,2,0:T(8,128)S(1)} custom-call(f32[1,64,64]{2,1,0:T(8,128)S(1)} %get-tuple-element.20), custom_call_target="InvertDiagBlocksLowerTriangular" | custom-call | tf_op jit(solution)/shard_map/triangular_solve | solution.py:159
  292.4 1.6 fusion.40
  294.0 1.3 copy.82
  (66 shorter events, 7.6 us)
Async XLA Ops:
  0.6 12.7 %copy-start.3 = (f32[8]{0:T(128)S(1)}, f32[8]{0:T(128)}, u32[]{:S(2)}) copy-start(f32[8]{0:T(128)} %param.6) | copy-start | bytes 100
  0.6 12.7 %copy-start.2 = (s32[2,32,256]{2,1,0:T(8,128)S(1)}, s32[2,32,256]{2,1,0:T(8,128)}, u32[]{:S(2)}) copy-start(s32[2,32,256]{2,1,0:T(8,128)} %param.5) | copy-start | bytes 196612
  0.7 12.7 %copy-start.4 = (f32[8]{0:T(128)S(1)}, f32[8]{0:T(128)}, u32[]{:S(2)}) copy-start(f32[8]{0:T(128)} %param.7) | copy-start | bytes 100
  0.7 18.2 %copy-start.5 = (f32[8]{0:T(128)S(1)}, f32[8]{0:T(128)}, u32[]{:S(2)}) copy-start(f32[8]{0:T(128)} %param.8) | copy-start | bytes 100
  3.0 26.1 %all-to-all-start = ((f32[64,2,8,256]{3,2,1,0:T(8,128)}), f32[64,2,8,256]{3,2,1,0:T(8,128)S(1)}, u32[]{:S(2)}, u32[]{:S(2)}) async-start(f32[64,2,8,256]{3,2,1,0:T(8,128)} %slice.139), calls=%async_computation | async-start | bytes 2097152 | tf_op jit(solution)/shard_map/all_to_all | solution.py:133
  13.5 8.8 %collective-permute-start.1 = (f32[1,32,256]{2,1,0:T(8,128)S(1)}, f32[1,32,256]{2,1,0:T(8,128)S(1)}, u32[]{:S(2)}, u32[]{:S(2)}) collective-permute-start(f32[1,32,256]{2,1,0:T(8,128)S(1)} %get-tuple-element.43), channel_id=1, source_target_pairs={{1,0},{2,1},{3,2},{4,3},{5,4},{6,5},{7,6},{8,7},{9,8},{10,9},{11,1... | collective-permute-start | bytes 98312 | tf_op jit(solution)/shard_map/ppermute | solution.py:24
  14.8 11.0 %collective-permute-start = (f32[1,32,256]{2,1,0:T(8,128)S(1)}, f32[1,32,256]{2,1,0:T(8,128)S(1)}, u32[]{:S(2)}, u32[]{:S(2)}) collective-permute-start(f32[1,32,256]{2,1,0:T(8,128)S(1)} %get-tuple-element.42), channel_id=1, source_target_pairs={{0,1},{1,2},{2,3},{3,4},{4,5},{5,6},{6,7},{7,8},{8,9},{9,10},{10,1... | collective-permute-start | bytes 98312 | tf_op jit(solution)/shard_map/ppermute | solution.py:22
  29.5 14.6 %collective-permute-start.3 = (f32[2,8,1,32,256]{4,3,2,1,0:T(8,128)S(1)}, f32[2,8,1,32,256]{4,3,2,1,0:T(8,128)S(1)}, u32[]{:S(2)}, u32[]{:S(2)}) collective-permute-start(f32[2,8,1,32,256]{4,3,2,1,0:T(8,128)S(1)} %get-tuple-element.38), channel_id=1, source_target_pairs={{1,0},{2,1},{3,2},{4,3},{5,4},{6,5},{7,6},{8,7},{9,8},{10,9},{11,1... | collective-permute-start | bytes 1572872 | tf_op jit(solution)/shard_map/ppermute | solution.py:24
  30.8 23.7 %collective-permute-start.2 = (f32[2,8,1,32,256]{4,3,2,1,0:T(8,128)S(1)}, f32[2,8,1,32,256]{4,3,2,1,0:T(8,128)S(1)}, u32[]{:S(2)}, u32[]{:S(2)}) collective-permute-start(f32[2,8,1,32,256]{4,3,2,1,0:T(8,128)S(1)} %get-tuple-element.37), channel_id=1, source_target_pairs={{0,1},{1,2},{2,3},{3,4},{4,5},{5,6},{6,7},{7,8},{8,9},{9,10},{10,1... | collective-permute-start | bytes 1572872 | tf_op jit(solution)/shard_map/ppermute | solution.py:22
  57.6 16.0 %collective-permute-start.5 = (f32[2,8,1,32,256]{4,3,2,1,0:T(8,128)S(1)}, f32[2,8,1,32,256]{4,3,2,1,0:T(8,128)S(1)}, u32[]{:S(2)}, u32[]{:S(2)}) collective-permute-start(f32[2,8,1,32,256]{4,3,2,1,0:T(8,128)S(1)} %get-tuple-element.36), channel_id=1, source_target_pairs={{1,0},{2,1},{3,2},{4,3},{5,4},{6,5},{7,6},{8,7},{9,8},{10,9},{11,1... | collective-permute-start | bytes 1572872 | tf_op jit(solution)/shard_map/ppermute | solution.py:24
  58.9 26.6 %collective-permute-start.4 = (f32[2,8,1,32,256]{4,3,2,1,0:T(8,128)S(1)}, f32[2,8,1,32,256]{4,3,2,1,0:T(8,128)S(1)}, u32[]{:S(2)}, u32[]{:S(2)}) collective-permute-start(f32[2,8,1,32,256]{4,3,2,1,0:T(8,128)S(1)} %get-tuple-element.35), channel_id=1, source_target_pairs={{0,1},{1,2},{2,3},{3,4},{4,5},{5,6},{6,7},{7,8},{8,9},{9,10},{10,1... | collective-permute-start | bytes 1572872 | tf_op jit(solution)/shard_map/ppermute | solution.py:22
  87.3 7.8 %copy-start.1 = (f32[256,2,8,256]{3,2,1,0:T(8,128)S(1)}, f32[256,2,8,256]{3,2,1,0:T(8,128)}, u32[]{:S(2)}) copy-start(f32[256,2,8,256]{3,2,1,0:T(8,128)} %param.9) | copy-start | bytes 12582916
  88.6 35.6 %collective-permute-start.7 = (f32[2,8,1,32,256]{4,3,2,1,0:T(8,128)S(1)}, f32[2,8,1,32,256]{4,3,2,1,0:T(8,128)S(1)}, u32[]{:S(2)}, u32[]{:S(2)}) collective-permute-start(f32[2,8,1,32,256]{4,3,2,1,0:T(8,128)S(1)} %get-tuple-element.34), channel_id=1, source_target_pairs={{1,0},{2,1},{3,2},{4,3},{5,4},{6,5},{7,6},{8,7},{9,8},{10,9},{11,1... | collective-permute-start | bytes 1572872 | tf_op jit(solution)/shard_map/ppermute | solution.py:24
  89.9 34.3 %collective-permute-start.6 = (f32[2,8,1,32,256]{4,3,2,1,0:T(8,128)S(1)}, f32[2,8,1,32,256]{4,3,2,1,0:T(8,128)S(1)}, u32[]{:S(2)}, u32[]{:S(2)}) collective-permute-start(f32[2,8,1,32,256]{4,3,2,1,0:T(8,128)S(1)} %get-tuple-element.33), channel_id=1, source_target_pairs={{0,1},{1,2},{2,3},{3,4},{4,5},{5,6},{6,7},{7,8},{8,9},{9,10},{10,1... | collective-permute-start | bytes 1572872 | tf_op jit(solution)/shard_map/ppermute | solution.py:22
  103.3 18.7 %collective-permute-start.17 = (f32[256,256]{1,0:T(8,128)S(1)}, f32[256,256]{1,0:T(8,128)S(1)}, u32[]{:S(2)}, u32[]{:S(2)}) collective-permute-start(f32[256,256]{1,0:T(8,128)S(1)} %fusion.5), channel_id=1, source_target_pairs={{0,1},{1,0},{2,3},{3,2},{4,5},{5,4},{6,7},{7,6},{8,9},{9,8},{10,11... | collective-permute-start | bytes 786440 | tf_op jit(solution)/shard_map/ppermute | solution.py:38
  122.1 12.4 %collective-permute-start.18 = (f32[256,256]{1,0:T(8,128)S(1)}, f32[256,256]{1,0:T(8,128)S(1)}, u32[]{:S(2)}, u32[]{:S(2)}) collective-permute-start(f32[256,256]{1,0:T(8,128)S(1)} %add.238), channel_id=1, source_target_pairs={{0,2},{1,3},{2,0},{3,1},{4,6},{5,7},{6,4},{7,5},{8,10},{9,11},{10,... | collective-permute-start | bytes 786440 | tf_op jit(solution)/shard_map/ppermute | solution.py:38
  129.2 47.0 %all-to-all-start.1 = ((f32[16,2,32,256]{3,1,0,2:T(2,128)}), f32[16,2,32,256]{3,1,0,2:T(2,128)S(1)}, u32[]{:S(2)}, u32[]{:S(2)}) async-start(f32[16,2,32,256]{3,1,0,2:T(2,128)} %copy.68), calls=%async_computation.1 | async-start | bytes 2097152 | tf_op jit(solution)/shard_map/all_to_all | solution.py:143
  134.6 19.0 %collective-permute-start.19 = (f32[256,256]{1,0:T(8,128)S(1)}, f32[256,256]{1,0:T(8,128)S(1)}, u32[]{:S(2)}, u32[]{:S(2)}) collective-permute-start(f32[256,256]{1,0:T(8,128)S(1)} %add.239), channel_id=1, source_target_pairs={{0,4},{1,5},{2,6},{3,7},{4,0},{5,1},{6,2},{7,3},{8,12},{9,13},{10,... | collective-permute-start | bytes 786440 | tf_op jit(solution)/shard_map/ppermute | solution.py:38
  153.6 19.5 %collective-permute-start.20 = (f32[256,256]{1,0:T(8,128)S(1)}, f32[256,256]{1,0:T(8,128)S(1)}, u32[]{:S(2)}, u32[]{:S(2)}) collective-permute-start(f32[256,256]{1,0:T(8,128)S(1)} %add.240), channel_id=1, source_target_pairs={{0,8},{1,9},{2,10},{3,11},{4,12},{5,13},{6,14},{7,15},{8,0},{9,1},... | collective-permute-start | bytes 786440 | tf_op jit(solution)/shard_map/ppermute | solution.py:38
  173.1 14.5 %collective-permute-start.21 = (f32[256,256]{1,0:T(8,128)S(1)}, f32[256,256]{1,0:T(8,128)S(1)}, u32[]{:S(2)}, u32[]{:S(2)}) collective-permute-start(f32[256,256]{1,0:T(8,128)S(1)} %add.241), channel_id=1, source_target_pairs={{0,16},{1,17},{2,18},{3,19},{4,20},{5,21},{6,22},{7,23},{8,24},{9,... | collective-permute-start | bytes 786440 | tf_op jit(solution)/shard_map/ppermute | solution.py:38
  183.4 8.5 %collective-permute-start.8 = (f32[64,320]{0,1:T(8,128)S(1)}, f32[64,320]{0,1:T(8,128)S(1)}, u32[]{:S(2)}, u32[]{:S(2)}) collective-permute-start(f32[64,320]{0,1:T(8,128)S(1)} %pad_maximum_fusion.6), channel_id=1, source_target_pairs={{0,1},{1,0},{2,3},{3,2},{4,5},{5,4},{6,7},{7,6},{8,9},{9,8},{10,11... | collective-permute-start | bytes 245768 | tf_op jit(solution)/shard_map/ppermute | solution.py:38
  187.6 86.7 %copy-start = (f32[32,8,16,256]{3,1,2,0:T(8,128)S(1)}, f32[32,8,16,256]{3,1,2,0:T(8,128)}, u32[]{:S(2)}) copy-start(f32[32,8,16,256]{3,1,2,0:T(8,128)} %copy.92) | copy-start | bytes 12582916
  187.6 16.8 %collective-permute-start.22 = (f32[256,256]{1,0:T(8,128)S(1)}, f32[256,256]{1,0:T(8,128)S(1)}, u32[]{:S(2)}, u32[]{:S(2)}) collective-permute-start(f32[256,256]{1,0:T(8,128)S(1)} %add.242), channel_id=1, source_target_pairs={{0,32},{1,33},{2,34},{3,35},{4,36},{5,37},{6,38},{7,39},{8,40},{9,... | collective-permute-start | bytes 786440 | tf_op jit(solution)/shard_map/ppermute | solution.py:38
  192.0 6.1 %collective-permute-start.9 = (f32[64,320]{0,1:T(8,128)S(1)}, f32[64,320]{0,1:T(8,128)S(1)}, u32[]{:S(2)}, u32[]{:S(2)}) collective-permute-start(f32[64,320]{0,1:T(8,128)S(1)} %fusion.69), channel_id=1, source_target_pairs={{0,2},{1,3},{2,0},{3,1},{4,6},{5,7},{6,4},{7,5},{8,10},{9,11},{10,... | collective-permute-start | bytes 245768 | tf_op jit(solution)/shard_map/ppermute | solution.py:38
  198.1 12.2 %collective-permute-start.10 = (f32[64,320]{0,1:T(8,128)S(1)}, f32[64,320]{0,1:T(8,128)S(1)}, u32[]{:S(2)}, u32[]{:S(2)}) collective-permute-start(f32[64,320]{0,1:T(8,128)S(1)} %add.230), channel_id=1, source_target_pairs={{0,4},{1,5},{2,6},{3,7},{4,0},{5,1},{6,2},{7,3},{8,12},{9,13},{10,... | collective-permute-start | bytes 245768 | tf_op jit(solution)/shard_map/ppermute | solution.py:38
  204.5 27.2 %collective-permute-start.23 = (f32[256,256]{1,0:T(8,128)S(1)}, f32[256,256]{1,0:T(8,128)S(1)}, u32[]{:S(2)}, u32[]{:S(2)}) collective-permute-start(f32[256,256]{1,0:T(8,128)S(1)} %add.243), channel_id=1, source_target_pairs={{0,64},{1,65},{2,66},{3,67},{4,68},{5,69},{6,70},{7,71},{8,72},{9,... | collective-permute-start | bytes 786440 | tf_op jit(solution)/shard_map/ppermute | solution.py:38
  210.3 13.2 %collective-permute-start.11 = (f32[64,320]{0,1:T(8,128)S(1)}, f32[64,320]{0,1:T(8,128)S(1)}, u32[]{:S(2)}, u32[]{:S(2)}) collective-permute-start(f32[64,320]{0,1:T(8,128)S(1)} %add.231), channel_id=1, source_target_pairs={{0,8},{1,9},{2,10},{3,11},{4,12},{5,13},{6,14},{7,15},{8,0},{9,1},... | collective-permute-start | bytes 245768 | tf_op jit(solution)/shard_map/ppermute | solution.py:38
  223.5 6.1 %collective-permute-start.12 = (f32[64,320]{0,1:T(8,128)S(1)}, f32[64,320]{0,1:T(8,128)S(1)}, u32[]{:S(2)}, u32[]{:S(2)}) collective-permute-start(f32[64,320]{0,1:T(8,128)S(1)} %add.232), channel_id=1, source_target_pairs={{0,16},{1,17},{2,18},{3,19},{4,20},{5,21},{6,22},{7,23},{8,24},{9,... | collective-permute-start | bytes 245768 | tf_op jit(solution)/shard_map/ppermute | solution.py:38
  229.6 10.7 %collective-permute-start.13 = (f32[64,320]{0,1:T(8,128)S(1)}, f32[64,320]{0,1:T(8,128)S(1)}, u32[]{:S(2)}, u32[]{:S(2)}) collective-permute-start(f32[64,320]{0,1:T(8,128)S(1)} %add.233), channel_id=1, source_target_pairs={{0,32},{1,33},{2,34},{3,35},{4,36},{5,37},{6,38},{7,39},{8,40},{9,... | collective-permute-start | bytes 245768 | tf_op jit(solution)/shard_map/ppermute | solution.py:38
  231.7 31.4 %collective-permute-start.24 = (f32[256,256]{1,0:T(8,128)S(1)}, f32[256,256]{1,0:T(8,128)S(1)}, u32[]{:S(2)}, u32[]{:S(2)}) collective-permute-start(f32[256,256]{1,0:T(8,128)S(1)} %add.244), channel_id=1, source_target_pairs={{0,128},{1,129},{2,130},{3,131},{4,132},{5,133},{6,134},{7,135},{8... | collective-permute-start | bytes 786440 | tf_op jit(solution)/shard_map/ppermute | solution.py:38
  240.3 12.2 %collective-permute-start.14 = (f32[64,320]{0,1:T(8,128)S(1)}, f32[64,320]{0,1:T(8,128)S(1)}, u32[]{:S(2)}, u32[]{:S(2)}) collective-permute-start(f32[64,320]{0,1:T(8,128)S(1)} %add.234), channel_id=1, source_target_pairs={{0,64},{1,65},{2,66},{3,67},{4,68},{5,69},{6,70},{7,71},{8,72},{9,... | collective-permute-start | bytes 245768 | tf_op jit(solution)/shard_map/ppermute | solution.py:38
  252.6 5.4 %collective-permute-start.15 = (f32[64,320]{0,1:T(8,128)S(1)}, f32[64,320]{0,1:T(8,128)S(1)}, u32[]{:S(2)}, u32[]{:S(2)}) collective-permute-start(f32[64,320]{0,1:T(8,128)S(1)} %add.235), channel_id=1, source_target_pairs={{0,128},{1,129},{2,130},{3,131},{4,132},{5,133},{6,134},{7,135},{8... | collective-permute-start | bytes 245768 | tf_op jit(solution)/shard_map/ppermute | solution.py:38
  258.0 9.3 %collective-permute-start.16 = (f32[64,320]{0,1:T(8,128)S(1)}, f32[64,320]{0,1:T(8,128)S(1)}, u32[]{:S(2)}, u32[]{:S(2)}) collective-permute-start(f32[64,320]{0,1:T(8,128)S(1)} %add.236), channel_id=1, source_target_pairs={{0,256},{1,257},{2,258},{3,259},{4,260},{5,261},{6,262},{7,263},{8... | collective-permute-start | bytes 245768 | tf_op jit(solution)/shard_map/ppermute | solution.py:38
  263.1 10.6 %collective-permute-start.25 = (f32[256,256]{1,0:T(8,128)S(1)}, f32[256,256]{1,0:T(8,128)S(1)}, u32[]{:S(2)}, u32[]{:S(2)}) collective-permute-start(f32[256,256]{1,0:T(8,128)S(1)} %add.245), channel_id=1, source_target_pairs={{0,256},{1,257},{2,258},{3,259},{4,260},{5,261},{6,262},{7,263},{8... | collective-permute-start | bytes 786440 | tf_op jit(solution)/shard_map/ppermute | solution.py:38

commit v4 on v3

--- a/solution.py
+++ b/solution.py
@@ -100,8 +100,15 @@
 
 
 def products(left_side, right_side):
+    cells = tuple(range(1, left_side.ndim))
     return lax.dot_general(
-        left_side, right_side, (((1,), (1,)), ((), ())), precision=lax.Precision.HIGHEST
+        left_side, right_side, ((cells, cells), ((), ())), precision=lax.Precision.HIGHEST
+    )
+
+
+def expand(weights, fields):
+    return lax.dot_general(
+        weights, fields, (((1,), (0,)), ((), ())), precision=lax.Precision.HIGHEST
     )
 
 
@@ -118,10 +125,9 @@
     slab_x = prior_basis.shape[1]
     quarter = prior_basis.shape[2]
     depth = prior_basis.shape[3]
-    flat_basis = prior_basis.reshape(basis_count, slab_x * quarter * depth)
     cell_weight = 1.0 / (slab_x * quarter * depth * groups * lax.axis_size("space"))
     tail_columns = prior_basis[basis_count - new_count :]
-    basis_gram = allsum(products(flat_basis, flat_basis)) * cell_weight
+    basis_gram = allsum(products(prior_basis, prior_basis)) * cell_weight
     conduct = lookup(labels, conductance)
     capacity = lookup(labels, capacity_table)
     rimmed = padded_2(conduct, (("space", 0),), 1)
@@ -141,14 +147,14 @@
     fields = chebyshev(source, face_list, diagonal, padder)
     merged = fields.reshape(per_device * COLS, slab_x, full_y, depth)
     regrouped = lax.all_to_all(merged, "shift", split_axis=2, concat_axis=0, tiled=True)
-    columns = regrouped.reshape(new_count, slab_x * quarter * depth)
+    columns = regrouped.reshape(new_count, slab_x, quarter, depth)
     sums = allsum(
-        jnp.concatenate([products(columns, flat_basis), products(columns, columns)], axis=1)
+        jnp.concatenate([products(columns, prior_basis), products(columns, columns)], axis=1)
     ) * cell_weight
     first_proj = sums[:, :basis_count]
     second_proj = first_proj - matmul(first_proj, basis_gram)
     coefficients = first_proj + second_proj
-    columns = columns - matmul(coefficients, flat_basis)
+    columns = columns - expand(coefficients, prior_basis)
     gram_matrix = (
         sums[:, basis_count:]
         - products(coefficients, first_proj)
@@ -156,7 +162,9 @@
         + products(matmul(coefficients, basis_gram), coefficients)
     )
     factor = jnp.linalg.cholesky(gram_matrix)
-    orthonormal = lax.linalg.triangular_solve(factor, columns, left_side=True, lower=True)
+    orthonormal = lax.linalg.triangular_solve(
+        factor, columns.reshape(new_count, slab_x * quarter * depth), left_side=True, lower=True
+    )
     new_block = orthonormal.reshape(shifts_all, COLS, slab_x, quarter, depth)
     return (new_block, coefficients, factor)
 

time: 301 us -> 305 us (1.013)
  starting transfers between devices: 108 us -> 117 us
  local copies, waits for them, and re-layouts: 16 us -> 9.57 us
    ppermute x18, starting transfers between devices: 69.6 us -> 78.5 us  [allsum(): lax.ppermute(value, axes, [(i, i ^ mask) for i in range(total)])]
    unnamed x16 -> x15, local copies, waits for them, and re-layouts: 10.3 us -> 3.58 us
    dot_general x6 -> x7, matrix products: 15.5 us -> 20.4 us  [the longest x6 15.5 us: products(): lax.dot_general(left_side, right_side, ((cells, cells), ((), ())), precis...]
  transfers between devices with their start and end apart: 28 -> 28, of which waited for: 19 -> 19; matrix products, arithmetic and copies ran while one was open for 10% -> 7% of each run, Pallas kernels for 0% -> 0%
where the time goes in v4:
time: 305 us; the launch traced here: 299 us
  waiting for transfers between devices  125 us (41%)
  starting transfers between devices  117 us (38%)
  other arithmetic  23.1 us (8%)
  matrix products  23 us (8%)
  local copies, waits for them, and re-layouts  9.57 us (3%)
    ppermute x18, starting transfers between devices, allsum(): lax.ppermute(value, axes, [(i, i ^ mask) for i in range(total)])  78.5 us
    ppermute x18, waiting for transfers between devices, allsum(): lax.ppermute(value, axes, [(i, i ^ mask) for i in range(total)])  73.6 us
    ppermute x4, waiting for transfers between devices, padded_2(): lax.ppermute(tail, axis, [(i, (i + 1) % count) for i in range(ends)])  25.7 us
    ppermute x4, waiting for transfers between devices, padded_2(): lax.ppermute(head, axis, [((i + 1) % count, i) for i in range(ends)])  22.6 us
    ppermute x4, starting transfers between devices, padded_2(): lax.ppermute(tail, axis, [(i, (i + 1) % count) for i in range(ends)])  18 us
    dot_general x6, matrix products, products(): lax.dot_general(left_side, right_side, ((cells, cells), ((), ())), precis...  15.5 us
    all_to_all x1, starting transfers between devices, local(): lax.all_to_all(tail_columns, 'shift', split_axis=0, concat_axis=2, tiled=...  10.4 us
    another operation x3, other arithmetic, local(): factor = jnp.linalg.cholesky(gram_matrix)  6.52 us
  transfers between devices with their start and end apart: 28, of which 19 were waited for; matrix products, arithmetic and copies ran while one was open for 7% of the time, Pallas kernels for 0%

profile of v4, /device:TPU:1, one launch (start us, length us, event | category | flops | bytes accessed | tf_op | source)
XLA Modules:
  0.0 299.3 jit_solution(2813028402223669971)
XLA Ops:
  0.7 2.3 slice.139
  3.0 10.4 %all-to-all-start = ((f32[64,2,8,256]{3,2,1,0:T(8,128)}), f32[64,2,8,256]{3,2,1,0:T(8,128)S(1)}, u32[]{:S(2)}, u32[]{:S(2)}) async-start(f32[64,2,8,256]{3,2,1,0:T(8,128)} %slice.139), calls=%async_computation | async-start | bytes 2097152 | tf_op jit(solution)/shard_map/all_to_all | solution.py:139
  13.5 1.3 collective-permute-start.1
  14.8 4.0 %collective-permute-start = (f32[1,32,256]{2,1,0:T(8,128)S(1)}, f32[1,32,256]{2,1,0:T(8,128)S(1)}, u32[]{:S(2)}, u32[]{:S(2)}) collective-permute-start(f32[1,32,256]{2,1,0:T(8,128)S(1)} %get-tuple-element.42), channel_id=1, source_target_pairs={{0,1},{1,2},{2,3},{3,4},{4,5},{5,6},{6,7},{7,8},{8,9},{9,10},{10,1... | collective-permute-start | bytes 98312 | tf_op jit(solution)/shard_map/ppermute | solution.py:22
  18.9 3.4 %collective-permute-done.1 = f32[1,32,256]{2,1,0:T(8,128)S(1)} collective-permute-done((f32[1,32,256]{2,1,0:T(8,128)S(1)}, f32[1,32,256]{2,1,0:T(8,128)S(1)}, u32[]{:S(2)}, u32[]{:S(2)}) %collective-permute-start.1) | collective-permute-done | bytes 32800 | tf_op jit(solution)/shard_map/ppermute | solution.py:24
  22.4 3.4 %collective-permute-done = f32[1,32,256]{2,1,0:T(8,128)S(1)} collective-permute-done((f32[1,32,256]{2,1,0:T(8,128)S(1)}, f32[1,32,256]{2,1,0:T(8,128)S(1)}, u32[]{:S(2)}, u32[]{:S(2)}) %collective-permute-start) | collective-permute-done | bytes 32800 | tf_op jit(solution)/shard_map/ppermute | solution.py:22
  26.2 2.9 all-to-all-done
  29.5 1.3 collective-permute-start.3
  30.8 4.0 %collective-permute-start.2 = (f32[2,8,1,32,256]{4,3,2,1,0:T(8,128)S(1)}, f32[2,8,1,32,256]{4,3,2,1,0:T(8,128)S(1)}, u32[]{:S(2)}, u32[]{:S(2)}) collective-permute-start(f32[2,8,1,32,256]{4,3,2,1,0:T(8,128)S(1)} %get-tuple-element.37), channel_id=1, source_target_pairs={{0,1},{1,2},{2,3},{3,4},{4,5},{5,6},{6,7},{7,8},{8,9},{9,10},{10,1... | collective-permute-start | bytes 1572872 | tf_op jit(solution)/shard_map/ppermute | solution.py:22
  34.8 9.2 %collective-permute-done.3 = f32[2,8,1,32,256]{4,3,2,1,0:T(8,128)S(1)} collective-permute-done((f32[2,8,1,32,256]{4,3,2,1,0:T(8,128)S(1)}, f32[2,8,1,32,256]{4,3,2,1,0:T(8,128)S(1)}, u32[]{:S(2)}, u32[]{:S(2)}) %collective-permute-start.3) | collective-permute-done | bytes 524320 | tf_op jit(solution)/shard_map/ppermute | solution.py:24
  44.0 10.4 %collective-permute-done.2 = f32[2,8,1,32,256]{4,3,2,1,0:T(8,128)S(1)} collective-permute-done((f32[2,8,1,32,256]{4,3,2,1,0:T(8,128)S(1)}, f32[2,8,1,32,256]{4,3,2,1,0:T(8,128)S(1)}, u32[]{:S(2)}, u32[]{:S(2)}) %collective-permute-start.2) | collective-permute-done | bytes 524320 | tf_op jit(solution)/shard_map/ppermute | solution.py:22
  54.4 1.8 select_maximum_fusion.4
  56.2 1.3 multiply_add_fusion.1
  57.6 1.3 collective-permute-start.5
  58.9 4.8 %collective-permute-start.4 = (f32[2,8,1,32,256]{4,3,2,1,0:T(8,128)S(1)}, f32[2,8,1,32,256]{4,3,2,1,0:T(8,128)S(1)}, u32[]{:S(2)}, u32[]{:S(2)}) collective-permute-start(f32[2,8,1,32,256]{4,3,2,1,0:T(8,128)S(1)} %get-tuple-element.35), channel_id=1, source_target_pairs={{0,1},{1,2},{2,3},{3,4},{4,5},{5,6},{6,7},{7,8},{8,9},{9,10},{10,1... | collective-permute-start | bytes 1572872 | tf_op jit(solution)/shard_map/ppermute | solution.py:22
  63.7 9.9 %collective-permute-done.5 = f32[2,8,1,32,256]{4,3,2,1,0:T(8,128)S(1)} collective-permute-done((f32[2,8,1,32,256]{4,3,2,1,0:T(8,128)S(1)}, f32[2,8,1,32,256]{4,3,2,1,0:T(8,128)S(1)}, u32[]{:S(2)}, u32[]{:S(2)}) %collective-permute-start.5) | collective-permute-done | bytes 524320 | tf_op jit(solution)/shard_map/ppermute | solution.py:24
  73.6 11.9 %collective-permute-done.4 = f32[2,8,1,32,256]{4,3,2,1,0:T(8,128)S(1)} collective-permute-done((f32[2,8,1,32,256]{4,3,2,1,0:T(8,128)S(1)}, f32[2,8,1,32,256]{4,3,2,1,0:T(8,128)S(1)}, u32[]{:S(2)}, u32[]{:S(2)}) %collective-permute-start.4) | collective-permute-done | bytes 524320 | tf_op jit(solution)/shard_map/ppermute | solution.py:22
  85.5 1.8 select_maximum_fusion.2
  87.4 1.2 multiply_add_fusion
  88.7 1.3 collective-permute-start.7
  90.0 5.2 %collective-permute-start.6 = (f32[2,8,1,32,256]{4,3,2,1,0:T(8,128)S(1)}, f32[2,8,1,32,256]{4,3,2,1,0:T(8,128)S(1)}, u32[]{:S(2)}, u32[]{:S(2)}) collective-permute-start(f32[2,8,1,32,256]{4,3,2,1,0:T(8,128)S(1)} %get-tuple-element.33), channel_id=1, source_target_pairs={{0,1},{1,2},{2,3},{3,4},{4,5},{5,6},{6,7},{7,8},{8,9},{9,10},{10,1... | collective-permute-start | bytes 1572872 | tf_op jit(solution)/shard_map/ppermute | solution.py:22
  95.2 8.2 %fusion.12 = f32[256,256]{1,0:T(8,128)S(1)} fusion(f32[256,2,8,256]{3,2,1,0:T(8,128)S(1)} %copy-done), kind=kOutput, calls=%fused_computation.20 | convolution fusion | flops 3221225472 | bytes 4456448 | tf_op jit(solution)/shard_map/dot_general | solution.py:104
  103.4 4.2 %collective-permute-start.17 = (f32[256,256]{1,0:T(8,128)S(1)}, f32[256,256]{1,0:T(8,128)S(1)}, u32[]{:S(2)}, u32[]{:S(2)}) collective-permute-start(f32[256,256]{1,0:T(8,128)S(1)} %fusion.12), channel_id=1, source_target_pairs={{0,1},{1,0},{2,3},{3,2},{4,5},{5,4},{6,7},{7,6},{8,9},{9,8},{10,11... | collective-permute-start | bytes 786440 | tf_op jit(solution)/shard_map/ppermute | solution.py:38
  107.7 14.5 %collective-permute-done.17 = f32[256,256]{1,0:T(8,128)S(1)} collective-permute-done((f32[256,256]{1,0:T(8,128)S(1)}, f32[256,256]{1,0:T(8,128)S(1)}, u32[]{:S(2)}, u32[]{:S(2)}) %collective-permute-start.17) | collective-permute-done | bytes 262176 | tf_op jit(solution)/shard_map/ppermute | solution.py:38
  122.2 2.1 collective-permute-start.18
  124.3 1.8 select_maximum_fusion
  126.1 1.4 fusion.25
  127.5 1.8 copy.82
  129.3 5.3 %all-to-all-start.1 = ((f32[16,2,32,256]{3,1,0,2:T(2,128)}), f32[16,2,32,256]{3,1,0,2:T(2,128)S(1)}, u32[]{:S(2)}, u32[]{:S(2)}) async-start(f32[16,2,32,256]{3,1,0,2:T(2,128)} %copy.82), calls=%async_computation.1 | async-start | bytes 2097152 | tf_op jit(solution)/shard_map/all_to_all | solution.py:149
  134.6 7.1 %collective-permute-start.19 = (f32[256,256]{1,0:T(8,128)S(1)}, f32[256,256]{1,0:T(8,128)S(1)}, u32[]{:S(2)}, u32[]{:S(2)}) collective-permute-start(f32[256,256]{1,0:T(8,128)S(1)} %add.239), channel_id=1, source_target_pairs={{0,4},{1,5},{2,6},{3,7},{4,0},{5,1},{6,2},{7,3},{8,12},{9,13},{10,... | collective-permute-start | bytes 786440 | tf_op jit(solution)/shard_map/ppermute | solution.py:38
  141.7 11.9 %collective-permute-done.19 = f32[256,256]{1,0:T(8,128)S(1)} collective-permute-done((f32[256,256]{1,0:T(8,128)S(1)}, f32[256,256]{1,0:T(8,128)S(1)}, u32[]{:S(2)}, u32[]{:S(2)}) %collective-permute-start.19) | collective-permute-done | bytes 262176 | tf_op jit(solution)/shard_map/ppermute | solution.py:38
  153.6 7.5 %collective-permute-start.20 = (f32[256,256]{1,0:T(8,128)S(1)}, f32[256,256]{1,0:T(8,128)S(1)}, u32[]{:S(2)}, u32[]{:S(2)}) collective-permute-start(f32[256,256]{1,0:T(8,128)S(1)} %add.240), channel_id=1, source_target_pairs={{0,8},{1,9},{2,10},{3,11},{4,12},{5,13},{6,14},{7,15},{8,0},{9,1},... | collective-permute-start | bytes 786440 | tf_op jit(solution)/shard_map/ppermute | solution.py:38
  161.2 11.9 %collective-permute-done.20 = f32[256,256]{1,0:T(8,128)S(1)} collective-permute-done((f32[256,256]{1,0:T(8,128)S(1)}, f32[256,256]{1,0:T(8,128)S(1)}, u32[]{:S(2)}, u32[]{:S(2)}) %collective-permute-start.20) | collective-permute-done | bytes 262176 | tf_op jit(solution)/shard_map/ppermute | solution.py:38
  173.2 3.2 %collective-permute-start.21 = (f32[256,256]{1,0:T(8,128)S(1)}, f32[256,256]{1,0:T(8,128)S(1)}, u32[]{:S(2)}, u32[]{:S(2)}) collective-permute-start(f32[256,256]{1,0:T(8,128)S(1)} %add.241), channel_id=1, source_target_pairs={{0,16},{1,17},{2,18},{3,19},{4,20},{5,21},{6,22},{7,23},{8,24},{9,... | collective-permute-start | bytes 786440 | tf_op jit(solution)/shard_map/ppermute | solution.py:38
  177.6 0.9 copy-done.1
  178.5 5.2 %fusion.16 = f32[64,256]{0,1:T(8,128)S(1)} fusion(f32[64,2,8,256]{3,0,2,1:T(8,128)S(1)} %bitcast.57, f32[256,2,8,256]{3,2,1,0:T(8,128)S(1)} %copy-done.1), kind=kOutput, calls=%fused_computation.23 | convolution fusion | flops 805306368 | bytes 5308416 | tf_op jit(solution)/shard_map/dot_general | solution.py:104
  183.7 1.0 convolution_bitcast_fusion
  184.7 4.1 %collective-permute-start.8 = (f32[64,320]{0,1:T(8,128)S(1)}, f32[64,320]{0,1:T(8,128)S(1)}, u32[]{:S(2)}, u32[]{:S(2)}) collective-permute-start(f32[64,320]{0,1:T(8,128)S(1)} %pad_maximum_fusion.6), channel_id=1, source_target_pairs={{0,1},{1,0},{2,3},{3,2},{4,5},{5,4},{6,7},{7,6},{8,9},{9,8},{10,11... | collective-permute-start | bytes 245768 | tf_op jit(solution)/shard_map/ppermute | solution.py:38
  188.9 4.1 %collective-permute-start.22 = (f32[256,256]{1,0:T(8,128)S(1)}, f32[256,256]{1,0:T(8,128)S(1)}, u32[]{:S(2)}, u32[]{:S(2)}) collective-permute-start(f32[256,256]{1,0:T(8,128)S(1)} %add.242), channel_id=1, source_target_pairs={{0,32},{1,33},{2,34},{3,35},{4,36},{5,37},{6,38},{7,39},{8,40},{9,... | collective-permute-start | bytes 786440 | tf_op jit(solution)/shard_map/ppermute | solution.py:38
  193.0 1.9 collective-permute-start.9
  195.0 4.1 %collective-permute-done.9 = f32[64,320]{0,1:T(8,128)S(1)} collective-permute-done((f32[64,320]{0,1:T(8,128)S(1)}, f32[64,320]{0,1:T(8,128)S(1)}, u32[]{:S(2)}, u32[]{:S(2)}) %collective-permute-start.9) | collective-permute-done | bytes 81952 | tf_op jit(solution)/shard_map/ppermute | solution.py:38
  199.1 2.9 collective-permute-start.10
  202.0 3.4 %collective-permute-done.22 = f32[256,256]{1,0:T(8,128)S(1)} collective-permute-done((f32[256,256]{1,0:T(8,128)S(1)}, f32[256,256]{1,0:T(8,128)S(1)}, u32[]{:S(2)}, u32[]{:S(2)}) %collective-permute-start.22) | collective-permute-done | bytes 262176 | tf_op jit(solution)/shard_map/ppermute | solution.py:38
  205.5 5.8 %collective-permute-start.23 = (f32[256,256]{1,0:T(8,128)S(1)}, f32[256,256]{1,0:T(8,128)S(1)}, u32[]{:S(2)}, u32[]{:S(2)}) collective-permute-start(f32[256,256]{1,0:T(8,128)S(1)} %add.243), channel_id=1, source_target_pairs={{0,64},{1,65},{2,66},{3,67},{4,68},{5,69},{6,70},{7,71},{8,72},{9,... | collective-permute-start | bytes 786440 | tf_op jit(solution)/shard_map/ppermute | solution.py:38
  211.3 4.3 %collective-permute-start.11 = (f32[64,320]{0,1:T(8,128)S(1)}, f32[64,320]{0,1:T(8,128)S(1)}, u32[]{:S(2)}, u32[]{:S(2)}) collective-permute-start(f32[64,320]{0,1:T(8,128)S(1)} %add.231), channel_id=1, source_target_pairs={{0,8},{1,9},{2,10},{3,11},{4,12},{5,13},{6,14},{7,15},{8,0},{9,1},... | collective-permute-start | bytes 245768 | tf_op jit(solution)/shard_map/ppermute | solution.py:38
  215.6 8.3 %collective-permute-done.11 = f32[64,320]{0,1:T(8,128)S(1)} collective-permute-done((f32[64,320]{0,1:T(8,128)S(1)}, f32[64,320]{0,1:T(8,128)S(1)}, u32[]{:S(2)}, u32[]{:S(2)}) %collective-permute-start.11) | collective-permute-done | bytes 81952 | tf_op jit(solution)/shard_map/ppermute | solution.py:38
  223.9 1.9 collective-permute-start.12
  225.9 4.1 %collective-permute-done.12 = f32[64,320]{0,1:T(8,128)S(1)} collective-permute-done((f32[64,320]{0,1:T(8,128)S(1)}, f32[64,320]{0,1:T(8,128)S(1)}, u32[]{:S(2)}, u32[]{:S(2)}) %collective-permute-start.12) | collective-permute-done | bytes 81952 | tf_op jit(solution)/shard_map/ppermute | solution.py:38
  230.0 3.0 %collective-permute-start.13 = (f32[64,320]{0,1:T(8,128)S(1)}, f32[64,320]{0,1:T(8,128)S(1)}, u32[]{:S(2)}, u32[]{:S(2)}) collective-permute-start(f32[64,320]{0,1:T(8,128)S(1)} %add.233), channel_id=1, source_target_pairs={{0,32},{1,33},{2,34},{3,35},{4,36},{5,37},{6,38},{7,39},{8,40},{9,... | collective-permute-start | bytes 245768 | tf_op jit(solution)/shard_map/ppermute | solution.py:38
  233.1 4.9 %collective-permute-start.24 = (f32[256,256]{1,0:T(8,128)S(1)}, f32[256,256]{1,0:T(8,128)S(1)}, u32[]{:S(2)}, u32[]{:S(2)}) collective-permute-start(f32[256,256]{1,0:T(8,128)S(1)} %add.244), channel_id=1, source_target_pairs={{0,128},{1,129},{2,130},{3,131},{4,132},{5,133},{6,134},{7,135},{8... | collective-permute-start | bytes 786440 | tf_op jit(solution)/shard_map/ppermute | solution.py:38
  238.5 5.0 %collective-permute-start.14 = (f32[64,320]{0,1:T(8,128)S(1)}, f32[64,320]{0,1:T(8,128)S(1)}, u32[]{:S(2)}, u32[]{:S(2)}) collective-permute-start(f32[64,320]{0,1:T(8,128)S(1)} %add.234), channel_id=1, source_target_pairs={{0,64},{1,65},{2,66},{3,67},{4,68},{5,69},{6,70},{7,71},{8,72},{9,... | collective-permute-start | bytes 245768 | tf_op jit(solution)/shard_map/ppermute | solution.py:38
  243.5 5.1 %collective-permute-done.14 = f32[64,320]{0,1:T(8,128)S(1)} collective-permute-done((f32[64,320]{0,1:T(8,128)S(1)}, f32[64,320]{0,1:T(8,128)S(1)}, u32[]{:S(2)}, u32[]{:S(2)}) %collective-permute-start.14) | collective-permute-done | bytes 81952 | tf_op jit(solution)/shard_map/ppermute | solution.py:38
  248.6 9.4 %collective-permute-start.15 = (f32[64,320]{0,1:T(8,128)S(1)}, f32[64,320]{0,1:T(8,128)S(1)}, u32[]{:S(2)}, u32[]{:S(2)}) collective-permute-start(f32[64,320]{0,1:T(8,128)S(1)} %add.235), channel_id=1, source_target_pairs={{0,128},{1,129},{2,130},{3,131},{4,132},{5,133},{6,134},{7,135},{8... | collective-permute-start | bytes 245768 | tf_op jit(solution)/shard_map/ppermute | solution.py:38
  258.0 1.0 collective-permute-done.15
  259.0 5.2 %collective-permute-start.16 = (f32[64,320]{0,1:T(8,128)S(1)}, f32[64,320]{0,1:T(8,128)S(1)}, u32[]{:S(2)}, u32[]{:S(2)}) collective-permute-start(f32[64,320]{0,1:T(8,128)S(1)} %add.236), channel_id=1, source_target_pairs={{0,256},{1,257},{2,258},{3,259},{4,260},{5,261},{6,262},{7,263},{8... | collective-permute-start | bytes 245768 | tf_op jit(solution)/shard_map/ppermute | solution.py:38
  264.3 1.9 collective-permute-start.25
  266.2 2.3 collective-permute-done.16
  268.5 6.4 %collective-permute-done.25 = f32[256,256]{1,0:T(8,128)S(1)} collective-permute-done((f32[256,256]{1,0:T(8,128)S(1)}, f32[256,256]{1,0:T(8,128)S(1)}, u32[]{:S(2)}, u32[]{:S(2)}) %collective-permute-start.25) | collective-permute-done | bytes 262176 | tf_op jit(solution)/shard_map/ppermute | solution.py:38
  275.5 5.0 %fusion.9 = f32[64,2,8,256]{3,0,2,1:T(8,128)S(1)} fusion(f32[64,2,8,256]{3,0,2,1:T(8,128)S(1)} %bitcast.59, f32[256,2,8,256]{3,2,1,0:T(8,128)S(1)} %copy-done.1, f32[64,256]{0,1:T(8,128)S(1)} %fusion.15), kind=kOutput, calls=%fused_computation.19 | convolution fusion | flops 805568512 | bytes 6356992 | tf_op jit(solution)/shard_map/dot_general | solution.py:110
  283.4 5.8 %cholesky.16 = f32[64,64]{1,0:T(8,128)S(1)} custom-call(f32[64,64]{1,0:T(8,128)S(1)} %fusion.77), custom_call_target="Cholesky" | custom-call | tf_op jit(solution)/shard_map/jit(cholesky)/cholesky | solution.py:164
  289.9 1.3 select_bitcast_fusion
  291.2 4.9 %custom-call.6 = f32[1,64,64]{1,2,0:T(8,128)S(1)} custom-call(f32[1,64,64]{2,1,0:T(8,128)S(1)} %get-tuple-element.20), custom_call_target="InvertDiagBlocksLowerTriangular" | custom-call | tf_op jit(solution)/shard_map/triangular_solve | solution.py:165
  296.2 1.6 fusion.50
  297.8 1.3 copy.100
  (64 shorter events, 7.7 us)
Async XLA Ops:
  0.6 12.7 %copy-start.3 = (f32[8]{0:T(128)S(1)}, f32[8]{0:T(128)}, u32[]{:S(2)}) copy-start(f32[8]{0:T(128)} %param.6) | copy-start | bytes 100
  0.6 12.7 %copy-start.2 = (s32[2,32,256]{2,1,0:T(8,128)S(1)}, s32[2,32,256]{2,1,0:T(8,128)}, u32[]{:S(2)}) copy-start(s32[2,32,256]{2,1,0:T(8,128)} %param.5) | copy-start | bytes 196612
  0.7 12.7 %copy-start.4 = (f32[8]{0:T(128)S(1)}, f32[8]{0:T(128)}, u32[]{:S(2)}) copy-start(f32[8]{0:T(128)} %param.7) | copy-start | bytes 100
  0.7 18.2 %copy-start.5 = (f32[8]{0:T(128)S(1)}, f32[8]{0:T(128)}, u32[]{:S(2)}) copy-start(f32[8]{0:T(128)} %param.8) | copy-start | bytes 100
  3.0 26.1 %all-to-all-start = ((f32[64,2,8,256]{3,2,1,0:T(8,128)}), f32[64,2,8,256]{3,2,1,0:T(8,128)S(1)}, u32[]{:S(2)}, u32[]{:S(2)}) async-start(f32[64,2,8,256]{3,2,1,0:T(8,128)} %slice.139), calls=%async_computation | async-start | bytes 2097152 | tf_op jit(solution)/shard_map/all_to_all | solution.py:139
  13.5 8.8 %collective-permute-start.1 = (f32[1,32,256]{2,1,0:T(8,128)S(1)}, f32[1,32,256]{2,1,0:T(8,128)S(1)}, u32[]{:S(2)}, u32[]{:S(2)}) collective-permute-start(f32[1,32,256]{2,1,0:T(8,128)S(1)} %get-tuple-element.43), channel_id=1, source_target_pairs={{1,0},{2,1},{3,2},{4,3},{5,4},{6,5},{7,6},{8,7},{9,8},{10,9},{11,1... | collective-permute-start | bytes 98312 | tf_op jit(solution)/shard_map/ppermute | solution.py:24
  14.8 11.0 %collective-permute-start = (f32[1,32,256]{2,1,0:T(8,128)S(1)}, f32[1,32,256]{2,1,0:T(8,128)S(1)}, u32[]{:S(2)}, u32[]{:S(2)}) collective-permute-start(f32[1,32,256]{2,1,0:T(8,128)S(1)} %get-tuple-element.42), channel_id=1, source_target_pairs={{0,1},{1,2},{2,3},{3,4},{4,5},{5,6},{6,7},{7,8},{8,9},{9,10},{10,1... | collective-permute-start | bytes 98312 | tf_op jit(solution)/shard_map/ppermute | solution.py:22
  29.5 14.6 %collective-permute-start.3 = (f32[2,8,1,32,256]{4,3,2,1,0:T(8,128)S(1)}, f32[2,8,1,32,256]{4,3,2,1,0:T(8,128)S(1)}, u32[]{:S(2)}, u32[]{:S(2)}) collective-permute-start(f32[2,8,1,32,256]{4,3,2,1,0:T(8,128)S(1)} %get-tuple-element.38), channel_id=1, source_target_pairs={{1,0},{2,1},{3,2},{4,3},{5,4},{6,5},{7,6},{8,7},{9,8},{10,9},{11,1... | collective-permute-start | bytes 1572872 | tf_op jit(solution)/shard_map/ppermute | solution.py:24
  30.8 23.7 %collective-permute-start.2 = (f32[2,8,1,32,256]{4,3,2,1,0:T(8,128)S(1)}, f32[2,8,1,32,256]{4,3,2,1,0:T(8,128)S(1)}, u32[]{:S(2)}, u32[]{:S(2)}) collective-permute-start(f32[2,8,1,32,256]{4,3,2,1,0:T(8,128)S(1)} %get-tuple-element.37), channel_id=1, source_target_pairs={{0,1},{1,2},{2,3},{3,4},{4,5},{5,6},{6,7},{7,8},{8,9},{9,10},{10,1... | collective-permute-start | bytes 1572872 | tf_op jit(solution)/shard_map/ppermute | solution.py:22
  57.6 16.0 %collective-permute-start.5 = (f32[2,8,1,32,256]{4,3,2,1,0:T(8,128)S(1)}, f32[2,8,1,32,256]{4,3,2,1,0:T(8,128)S(1)}, u32[]{:S(2)}, u32[]{:S(2)}) collective-permute-start(f32[2,8,1,32,256]{4,3,2,1,0:T(8,128)S(1)} %get-tuple-element.36), channel_id=1, source_target_pairs={{1,0},{2,1},{3,2},{4,3},{5,4},{6,5},{7,6},{8,7},{9,8},{10,9},{11,1... | collective-permute-start | bytes 1572872 | tf_op jit(solution)/shard_map/ppermute | solution.py:24
  58.9 26.6 %collective-permute-start.4 = (f32[2,8,1,32,256]{4,3,2,1,0:T(8,128)S(1)}, f32[2,8,1,32,256]{4,3,2,1,0:T(8,128)S(1)}, u32[]{:S(2)}, u32[]{:S(2)}) collective-permute-start(f32[2,8,1,32,256]{4,3,2,1,0:T(8,128)S(1)} %get-tuple-element.35), channel_id=1, source_target_pairs={{0,1},{1,2},{2,3},{3,4},{4,5},{5,6},{6,7},{7,8},{8,9},{9,10},{10,1... | collective-permute-start | bytes 1572872 | tf_op jit(solution)/shard_map/ppermute | solution.py:22
  87.4 7.8 %copy-start = (f32[256,2,8,256]{3,2,1,0:T(8,128)S(1)}, f32[256,2,8,256]{3,2,1,0:T(8,128)}, u32[]{:S(2)}) copy-start(f32[256,2,8,256]{3,2,1,0:T(8,128)} %param.9) | copy-start | bytes 12582916
  88.7 35.6 %collective-permute-start.7 = (f32[2,8,1,32,256]{4,3,2,1,0:T(8,128)S(1)}, f32[2,8,1,32,256]{4,3,2,1,0:T(8,128)S(1)}, u32[]{:S(2)}, u32[]{:S(2)}) collective-permute-start(f32[2,8,1,32,256]{4,3,2,1,0:T(8,128)S(1)} %get-tuple-element.34), channel_id=1, source_target_pairs={{1,0},{2,1},{3,2},{4,3},{5,4},{6,5},{7,6},{8,7},{9,8},{10,9},{11,1... | collective-permute-start | bytes 1572872 | tf_op jit(solution)/shard_map/ppermute | solution.py:24
  90.0 34.3 %collective-permute-start.6 = (f32[2,8,1,32,256]{4,3,2,1,0:T(8,128)S(1)}, f32[2,8,1,32,256]{4,3,2,1,0:T(8,128)S(1)}, u32[]{:S(2)}, u32[]{:S(2)}) collective-permute-start(f32[2,8,1,32,256]{4,3,2,1,0:T(8,128)S(1)} %get-tuple-element.33), channel_id=1, source_target_pairs={{0,1},{1,2},{2,3},{3,4},{4,5},{5,6},{6,7},{7,8},{8,9},{9,10},{10,1... | collective-permute-start | bytes 1572872 | tf_op jit(solution)/shard_map/ppermute | solution.py:22
  103.4 18.7 %collective-permute-start.17 = (f32[256,256]{1,0:T(8,128)S(1)}, f32[256,256]{1,0:T(8,128)S(1)}, u32[]{:S(2)}, u32[]{:S(2)}) collective-permute-start(f32[256,256]{1,0:T(8,128)S(1)} %fusion.12), channel_id=1, source_target_pairs={{0,1},{1,0},{2,3},{3,2},{4,5},{5,4},{6,7},{7,6},{8,9},{9,8},{10,11... | collective-permute-start | bytes 786440 | tf_op jit(solution)/shard_map/ppermute | solution.py:38
  122.2 12.4 %collective-permute-start.18 = (f32[256,256]{1,0:T(8,128)S(1)}, f32[256,256]{1,0:T(8,128)S(1)}, u32[]{:S(2)}, u32[]{:S(2)}) collective-permute-start(f32[256,256]{1,0:T(8,128)S(1)} %add.238), channel_id=1, source_target_pairs={{0,2},{1,3},{2,0},{3,1},{4,6},{5,7},{6,4},{7,5},{8,10},{9,11},{10,... | collective-permute-start | bytes 786440 | tf_op jit(solution)/shard_map/ppermute | solution.py:38
  129.3 47.0 %all-to-all-start.1 = ((f32[16,2,32,256]{3,1,0,2:T(2,128)}), f32[16,2,32,256]{3,1,0,2:T(2,128)S(1)}, u32[]{:S(2)}, u32[]{:S(2)}) async-start(f32[16,2,32,256]{3,1,0,2:T(2,128)} %copy.82), calls=%async_computation.1 | async-start | bytes 2097152 | tf_op jit(solution)/shard_map/all_to_all | solution.py:149
  134.6 19.0 %collective-permute-start.19 = (f32[256,256]{1,0:T(8,128)S(1)}, f32[256,256]{1,0:T(8,128)S(1)}, u32[]{:S(2)}, u32[]{:S(2)}) collective-permute-start(f32[256,256]{1,0:T(8,128)S(1)} %add.239), channel_id=1, source_target_pairs={{0,4},{1,5},{2,6},{3,7},{4,0},{5,1},{6,2},{7,3},{8,12},{9,13},{10,... | collective-permute-start | bytes 786440 | tf_op jit(solution)/shard_map/ppermute | solution.py:38
  153.6 19.5 %collective-permute-start.20 = (f32[256,256]{1,0:T(8,128)S(1)}, f32[256,256]{1,0:T(8,128)S(1)}, u32[]{:S(2)}, u32[]{:S(2)}) collective-permute-start(f32[256,256]{1,0:T(8,128)S(1)} %add.240), channel_id=1, source_target_pairs={{0,8},{1,9},{2,10},{3,11},{4,12},{5,13},{6,14},{7,15},{8,0},{9,1},... | collective-permute-start | bytes 786440 | tf_op jit(solution)/shard_map/ppermute | solution.py:38
  173.2 15.7 %collective-permute-start.21 = (f32[256,256]{1,0:T(8,128)S(1)}, f32[256,256]{1,0:T(8,128)S(1)}, u32[]{:S(2)}, u32[]{:S(2)}) collective-permute-start(f32[256,256]{1,0:T(8,128)S(1)} %add.241), channel_id=1, source_target_pairs={{0,16},{1,17},{2,18},{3,19},{4,20},{5,21},{6,22},{7,23},{8,24},{9,... | collective-permute-start | bytes 786440 | tf_op jit(solution)/shard_map/ppermute | solution.py:38
  176.4 2.2 copy-start.1
  184.7 8.3 %collective-permute-start.8 = (f32[64,320]{0,1:T(8,128)S(1)}, f32[64,320]{0,1:T(8,128)S(1)}, u32[]{:S(2)}, u32[]{:S(2)}) collective-permute-start(f32[64,320]{0,1:T(8,128)S(1)} %pad_maximum_fusion.6), channel_id=1, source_target_pairs={{0,1},{1,0},{2,3},{3,2},{4,5},{5,4},{6,7},{7,6},{8,9},{9,8},{10,11... | collective-permute-start | bytes 245768 | tf_op jit(solution)/shard_map/ppermute | solution.py:38
  188.9 16.5 %collective-permute-start.22 = (f32[256,256]{1,0:T(8,128)S(1)}, f32[256,256]{1,0:T(8,128)S(1)}, u32[]{:S(2)}, u32[]{:S(2)}) collective-permute-start(f32[256,256]{1,0:T(8,128)S(1)} %add.242), channel_id=1, source_target_pairs={{0,32},{1,33},{2,34},{3,35},{4,36},{5,37},{6,38},{7,39},{8,40},{9,... | collective-permute-start | bytes 786440 | tf_op jit(solution)/shard_map/ppermute | solution.py:38
  193.0 6.1 %collective-permute-start.9 = (f32[64,320]{0,1:T(8,128)S(1)}, f32[64,320]{0,1:T(8,128)S(1)}, u32[]{:S(2)}, u32[]{:S(2)}) collective-permute-start(f32[64,320]{0,1:T(8,128)S(1)} %fusion.80), channel_id=1, source_target_pairs={{0,2},{1,3},{2,0},{3,1},{4,6},{5,7},{6,4},{7,5},{8,10},{9,11},{10,... | collective-permute-start | bytes 245768 | tf_op jit(solution)/shard_map/ppermute | solution.py:38
  199.1 12.2 %collective-permute-start.10 = (f32[64,320]{0,1:T(8,128)S(1)}, f32[64,320]{0,1:T(8,128)S(1)}, u32[]{:S(2)}, u32[]{:S(2)}) collective-permute-start(f32[64,320]{0,1:T(8,128)S(1)} %add.230), channel_id=1, source_target_pairs={{0,4},{1,5},{2,6},{3,7},{4,0},{5,1},{6,2},{7,3},{8,12},{9,13},{10,... | collective-permute-start | bytes 245768 | tf_op jit(solution)/shard_map/ppermute | solution.py:38
  205.5 27.6 %collective-permute-start.23 = (f32[256,256]{1,0:T(8,128)S(1)}, f32[256,256]{1,0:T(8,128)S(1)}, u32[]{:S(2)}, u32[]{:S(2)}) collective-permute-start(f32[256,256]{1,0:T(8,128)S(1)} %add.243), channel_id=1, source_target_pairs={{0,64},{1,65},{2,66},{3,67},{4,68},{5,69},{6,70},{7,71},{8,72},{9,... | collective-permute-start | bytes 786440 | tf_op jit(solution)/shard_map/ppermute | solution.py:38
  211.3 12.6 %collective-permute-start.11 = (f32[64,320]{0,1:T(8,128)S(1)}, f32[64,320]{0,1:T(8,128)S(1)}, u32[]{:S(2)}, u32[]{:S(2)}) collective-permute-start(f32[64,320]{0,1:T(8,128)S(1)} %add.231), channel_id=1, source_target_pairs={{0,8},{1,9},{2,10},{3,11},{4,12},{5,13},{6,14},{7,15},{8,0},{9,1},... | collective-permute-start | bytes 245768 | tf_op jit(solution)/shard_map/ppermute | solution.py:38
  223.9 6.1 %collective-permute-start.12 = (f32[64,320]{0,1:T(8,128)S(1)}, f32[64,320]{0,1:T(8,128)S(1)}, u32[]{:S(2)}, u32[]{:S(2)}) collective-permute-start(f32[64,320]{0,1:T(8,128)S(1)} %add.232), channel_id=1, source_target_pairs={{0,16},{1,17},{2,18},{3,19},{4,20},{5,21},{6,22},{7,23},{8,24},{9,... | collective-permute-start | bytes 245768 | tf_op jit(solution)/shard_map/ppermute | solution.py:38
  230.0 8.4 %collective-permute-start.13 = (f32[64,320]{0,1:T(8,128)S(1)}, f32[64,320]{0,1:T(8,128)S(1)}, u32[]{:S(2)}, u32[]{:S(2)}) collective-permute-start(f32[64,320]{0,1:T(8,128)S(1)} %add.233), channel_id=1, source_target_pairs={{0,32},{1,33},{2,34},{3,35},{4,36},{5,37},{6,38},{7,39},{8,40},{9,... | collective-permute-start | bytes 245768 | tf_op jit(solution)/shard_map/ppermute | solution.py:38
  233.1 31.1 %collective-permute-start.24 = (f32[256,256]{1,0:T(8,128)S(1)}, f32[256,256]{1,0:T(8,128)S(1)}, u32[]{:S(2)}, u32[]{:S(2)}) collective-permute-start(f32[256,256]{1,0:T(8,128)S(1)} %add.244), channel_id=1, source_target_pairs={{0,128},{1,129},{2,130},{3,131},{4,132},{5,133},{6,134},{7,135},{8... | collective-permute-start | bytes 786440 | tf_op jit(solution)/shard_map/ppermute | solution.py:38
  238.5 10.1 %collective-permute-start.14 = (f32[64,320]{0,1:T(8,128)S(1)}, f32[64,320]{0,1:T(8,128)S(1)}, u32[]{:S(2)}, u32[]{:S(2)}) collective-permute-start(f32[64,320]{0,1:T(8,128)S(1)} %add.234), channel_id=1, source_target_pairs={{0,64},{1,65},{2,66},{3,67},{4,68},{5,69},{6,70},{7,71},{8,72},{9,... | collective-permute-start | bytes 245768 | tf_op jit(solution)/shard_map/ppermute | solution.py:38
  248.6 10.4 %collective-permute-start.15 = (f32[64,320]{0,1:T(8,128)S(1)}, f32[64,320]{0,1:T(8,128)S(1)}, u32[]{:S(2)}, u32[]{:S(2)}) collective-permute-start(f32[64,320]{0,1:T(8,128)S(1)} %add.235), channel_id=1, source_target_pairs={{0,128},{1,129},{2,130},{3,131},{4,132},{5,133},{6,134},{7,135},{8... | collective-permute-start | bytes 245768 | tf_op jit(solution)/shard_map/ppermute | solution.py:38
  259.0 9.5 %collective-permute-start.16 = (f32[64,320]{0,1:T(8,128)S(1)}, f32[64,320]{0,1:T(8,128)S(1)}, u32[]{:S(2)}, u32[]{:S(2)}) collective-permute-start(f32[64,320]{0,1:T(8,128)S(1)} %add.236), channel_id=1, source_target_pairs={{0,256},{1,257},{2,258},{3,259},{4,260},{5,261},{6,262},{7,263},{8... | collective-permute-start | bytes 245768 | tf_op jit(solution)/shard_map/ppermute | solution.py:38
  264.3 10.6 %collective-permute-start.25 = (f32[256,256]{1,0:T(8,128)S(1)}, f32[256,256]{1,0:T(8,128)S(1)}, u32[]{:S(2)}, u32[]{:S(2)}) collective-permute-start(f32[256,256]{1,0:T(8,128)S(1)} %add.245), channel_id=1, source_target_pairs={{0,256},{1,257},{2,258},{3,259},{4,260},{5,261},{6,262},{7,263},{8... | collective-permute-start | bytes 786440 | tf_op jit(solution)/shard_map/ppermute | solution.py:38
